TPU v7x, 32 devices: a whole 2x2x4 slice. The times are simulated.
32 devices in a mesh: section: 4 (over y, x), expert: 8 (over z, core).
Axes of the slice: x: 2, y: 2, z: 4, core: 2. Of those that a mesh axis runs over, the one named last changes fastest.
Arguments:
- tokens: bfloat16 [4, 2, 256, 2048], P('section', None, 'expert'), may hold values from -6 to 6
- routes: int32 [4, 2, 256, 2], P('section', None, 'expert'), may hold values from 0 to 3, all different within a row; in each aligned block of 32 rows (0 to 31, 32 to 63, ..., all dimensions but the last counted through in order) at most 24 rows name the same one
- combine_weights: float32 [4, 2, 256, 2], P('section', None, 'expert'), may hold values from 0.3 to 1
- norm_gain: float32 [4, 2048], P('section'), may hold values from 0.5 to 1.5
- gate_up: bfloat16 [4, 8, 2048, 768], P('section', 'expert'), may hold values from -0.125 to 0.125
- down: bfloat16 [4, 8, 384, 2048], P('section', 'expert'), may hold values from -0.21875 to 0.21875
Outputs:
- next_inputs: bfloat16 [4, 2, 256, 2048], P('section', None, 'expert')
Inputs may be any that keep to these rules, and one draw needn't show every extreme that they name: `routes`: each token names 2 different experts. Among the 32 tokens of one device in one section and micro-batch (aligned blocks of 32 rows) no expert is named more than 24 times.
All inputs are finite; a program needn't handle non-finite values.
Results may differ from a plain program's by a relative error of at most 0.0055.
Values may be sent and summed in bfloat16 or wider, within the bound.
No kernel may reach another device: no remote copies, remote signals or barrier semaphores. Data moves between devices by JAX's collectives and lax.ppermute only.
A program may use at most 64 MiB of HBM per device.

v0:
```python
import jax
import jax.numpy as jnp
from jax import lax
from jax.sharding import PartitionSpec as P

EPSILON = 1e-06


def from_behind(value, axis, steps):
    count = lax.axis_size(axis)
    pairs = [(source, (source + steps) % count) for source in range(count)]
    return lax.ppermute(value, axis, pairs)


def slot_codes(route_block, experts, capacity):
    flat = route_block.reshape(-1)
    onehot = (flat[:, None] == jnp.arange(experts, dtype=jnp.int32)[None, :]).astype(jnp.int32)
    before = jnp.cumsum(onehot, axis=0) - onehot
    slot = jnp.sum(before * onehot, axis=1)
    return (flat * capacity + slot).reshape(route_block.shape)


def normalize(block, gain):
    values = block.astype(jnp.float32)
    scale = lax.rsqrt(jnp.mean(values * values, axis=-1, keepdims=True) + EPSILON)
    return (values * scale * gain).astype(jnp.bfloat16)


def expert_half(block, weights_gu, weights_dn):
    shape = block.shape
    token_rows = block.reshape(-1, shape[-1])
    units = weights_dn.shape[0]
    joined = jnp.dot(token_rows, weights_gu, preferred_element_type=jnp.float32)
    hidden = (jax.nn.silu(joined[:, :units]) * joined[:, units:]).astype(jnp.bfloat16)
    partial_out = jnp.dot(hidden, weights_dn, preferred_element_type=jnp.float32).astype(
        jnp.bfloat16
    )
    return partial_out.reshape(shape)


def handoff(layer_out):
    return from_behind(layer_out, "section", 1)


def local(tokens, routes, combine_weights, norm_gain, gate_up, down):
    experts = lax.axis_size("expert") // 2
    tok_count = tokens.shape[2]
    width = tokens.shape[3]
    topk = routes.shape[3]
    capacity = 2 * ((3 * tok_count * topk + 4 * experts - 1) // (4 * experts))
    weights_gu = gate_up[0, 0]
    weights_dn = down[0, 0]
    gain = norm_gain[0]
    inputs = tokens[0]
    choices_in = routes[0]
    weights_in = combine_weights[0]
    pieces = []
    for position in range(inputs.shape[0]):
        section_x = inputs[position : position + 1]
        count = section_x.shape[0]
        normed = normalize(section_x, gain)
        codes = jax.vmap(lambda block: slot_codes(block, experts, capacity))(
            choices_in[position : position + 1]
        )
        lanes = jnp.arange(experts * capacity, dtype=jnp.int32)
        onehot = jnp.any(codes[..., None] == lanes, axis=2).astype(jnp.bfloat16)
        buffer = jnp.einsum("mtq,mtd->qmd", onehot, normed, preferred_element_type=jnp.float32)
        buffer = buffer.astype(jnp.bfloat16).reshape(experts, capacity, count, width)
        outgoing = jnp.repeat(buffer, 2, axis=0)
        incoming = lax.all_to_all(outgoing, "expert", split_axis=0, concat_axis=0, tiled=True)
        parts = expert_half(incoming, weights_gu, weights_dn)
        returned = lax.all_to_all(parts, "expert", split_axis=0, concat_axis=0, tiled=True)
        pairs = returned.reshape(experts, 2, capacity, count, width)
        results = (pairs[:, 0].astype(jnp.float32) + pairs[:, 1].astype(jnp.float32)).astype(
            jnp.bfloat16
        )
        table = jnp.swapaxes(results.reshape(experts * capacity, count, width), 0, 1)
        flat_codes = codes.reshape(count, tok_count * topk)
        picked = table[jnp.arange(count)[:, None], flat_codes].reshape(
            count, tok_count, topk, width
        )
        mixed = section_x.astype(jnp.float32) + jnp.sum(
            weights_in[position : position + 1][..., None] * picked.astype(jnp.float32), axis=2
        )
        finished_layer = mixed.astype(jnp.bfloat16)
        pieces.append(handoff(finished_layer))
    moved = jnp.concatenate(pieces, axis=0)
    return moved[None]


def solution(mesh):
    return jax.shard_map(
        local,
        mesh=mesh,
        in_specs=(
            P("section", None, "expert", None),
            P("section", None, "expert", None),
            P("section", None, "expert", None),
            P("section", None),
            P("section", "expert", None, None),
            P("section", "expert", None, None),
        ),
        out_specs=P("section", None, "expert", None),
        check_vma=False,
    )
```

profile of v0, /device:TPU:0, one launch (start us, length us, event | category | flops | bytes accessed | tf_op | source)
XLA Modules:
  0.0 130.0 jit_solution(14057331167735075358)
XLA Ops:
  4.3 1.3 convolution_convert_fusion.2
  6.6 6.4 %all-to-all-start.2 = ((bf16[8,24,1,2048]{3,1,2,0:T(8,128)(2,1)}), bf16[8,24,1,2048]{3,1,2,0:T(8,128)(2,1)}, u32[]{:S(2)}, u32[]{:S(2)}) async-start(bf16[8,24,1,2048]{3,1,2,0:T(8,128)(2,1)} %bitcast.133), calls=%async_computation.2 | async-start | bytes 1572864 | tf_op jit(solution)/shard_map/all_to_all | solution.py:70
  14.1 20.0 %all-to-all-done.2 = bf16[8,24,1,2048]{3,1,2,0:T(8,128)(2,1)} async-done(((bf16[8,24,1,2048]{3,1,2,0:T(8,128)(2,1)}), bf16[8,24,1,2048]{3,1,2,0:T(8,128)(2,1)}, u32[]{:S(2)}, u32[]{:S(2)}) %all-to-all-start.2) | async-done | bytes 786464 | tf_op jit(solution)/shard_map/all_to_all | solution.py:70
  34.0 2.0 %broadcast_in_dim.10 = bf16[4,2,24,2048]{3,2,1,0:T(8,128)(2,1)} broadcast(bf16[4,24,2048]{2,1,0:T(8,128)(2,1)} %bitcast.135), dimensions={0,2,3} | broadcast | bytes 1179648 | tf_op jit(solution)/shard_map/broadcast_in_dim | solution.py:69
  36.0 4.2 %all-to-all-start = ((bf16[8,24,1,2048]{3,1,2,0:T(8,128)(2,1)}), bf16[8,24,1,2048]{3,1,2,0:T(8,128)(2,1)}, u32[]{:S(2)}, u32[]{:S(2)}) async-start(bf16[8,24,1,2048]{3,1,2,0:T(8,128)(2,1)} %bitcast.134), calls=%async_computation | async-start | bytes 1572864 | tf_op jit(solution)/shard_map/all_to_all | solution.py:70
  40.2 2.0 %fusion = f32[192,768]{1,0:T(8,128)S(1)} fusion(bf16[192,2048]{1,0:T(8,128)(2,1)} %bitcast.28, bf16[1,1,2048,768]{3,2,1,0:T(8,128)(2,1)S(1)} %copy-done), kind=kOutput, calls=%fused_computation.2 | convolution fusion | flops 603979776 | bytes 4521984 | tf_op jit(solution)/shard_map/dot_general | solution.py:33
  42.3 1.5 %convolution_convert_fusion = bf16[192,2048]{1,0:T(8,128)(2,1)} fusion(bf16[1,1,384,2048]{3,2,1,0:T(8,128)(2,1)S(1)} %copy-done.6, f32[192,768]{1,0:T(8,128)S(1)} %fusion), kind=kOutput, calls=%fused_computation.6 | convolution fusion | flops 302825472 | bytes 2949120 | tf_op jit(solution)/shard_map/dot_general | solution.py:35
  43.8 17.4 %all-to-all-done = bf16[8,24,1,2048]{3,1,2,0:T(8,128)(2,1)} async-done(((bf16[8,24,1,2048]{3,1,2,0:T(8,128)(2,1)}), bf16[8,24,1,2048]{3,1,2,0:T(8,128)(2,1)}, u32[]{:S(2)}, u32[]{:S(2)}) %all-to-all-start) | async-done | bytes 786464 | tf_op jit(solution)/shard_map/all_to_all | solution.py:70
  61.2 4.2 %all-to-all-start.3 = ((bf16[8,24,1,2048]{3,1,2,0:T(8,128)(2,1)}), bf16[8,24,1,2048]{3,1,2,0:T(8,128)(2,1)}, u32[]{:S(2)}, u32[]{:S(2)}) async-start(bf16[8,24,1,2048]{3,1,2,0:T(8,128)(2,1)} %bitcast.138), calls=%async_computation.3 | async-start | bytes 1572864 | tf_op jit(solution)/shard_map/all_to_all | solution.py:72
  65.6 2.0 %fusion.2 = f32[192,768]{1,0:T(8,128)S(1)} fusion(bf16[192,2048]{1,0:T(8,128)(2,1)} %bitcast.9, bf16[1,1,2048,768]{3,2,1,0:T(8,128)(2,1)S(1)} %copy-done), kind=kOutput, calls=%fused_computation.4 | convolution fusion | flops 603979776 | bytes 4521984 | tf_op jit(solution)/shard_map/dot_general | solution.py:33
  67.6 1.5 %convolution_convert_fusion.1 = bf16[192,2048]{1,0:T(8,128)(2,1)} fusion(bf16[1,1,384,2048]{3,2,1,0:T(8,128)(2,1)S(1)} %copy-done.7, f32[192,768]{1,0:T(8,128)S(1)} %fusion.2), kind=kOutput, calls=%fused_computation.7 | convolution fusion | flops 302825472 | bytes 2949120 | tf_op jit(solution)/shard_map/dot_general | solution.py:35
  69.1 17.2 %all-to-all-done.3 = bf16[8,24,1,2048]{3,1,2,0:T(8,128)(2,1)} async-done(((bf16[8,24,1,2048]{3,1,2,0:T(8,128)(2,1)}), bf16[8,24,1,2048]{3,1,2,0:T(8,128)(2,1)}, u32[]{:S(2)}, u32[]{:S(2)}) %all-to-all-start.3) | async-done | bytes 786464 | tf_op jit(solution)/shard_map/all_to_all | solution.py:72
  86.3 4.2 %all-to-all-start.1 = ((bf16[8,24,1,2048]{3,1,2,0:T(8,128)(2,1)}), bf16[8,24,1,2048]{3,1,2,0:T(8,128)(2,1)}, u32[]{:S(2)}, u32[]{:S(2)}) async-start(bf16[8,24,1,2048]{3,1,2,0:T(8,128)(2,1)} %bitcast.137), calls=%async_computation.1 | async-start | bytes 1572864 | tf_op jit(solution)/shard_map/all_to_all | solution.py:72
  93.4 2.1 %gather_fusion.1 = bf16[64,2048]{1,0:T(8,128)(2,1)} fusion(bf16[1,96,2048]{2,1,0:T(8,128)(2,1)S(1)} %bitcast.131, s32[64]{0:T(128)S(1)} %or_bitcast_fusion), kind=kCustom, calls=%fused_computation.1 | custom fusion | bytes 524800 | tf_op jit(solution)/shard_map/gather | solution.py:79
  95.5 2.1 %reshape.660 = f32[1,32,2,2048]{3,2,1,0:T(2,128)} reshape(bf16[64,2048]{1,0:T(8,128)(2,1)} %gather_fusion.1) | data formatting | bytes 786432 | tf_op jit(solution)/shard_map/convert_element_type | solution.py:83
  97.6 13.9 %all-to-all-done.1 = bf16[8,24,1,2048]{3,1,2,0:T(8,128)(2,1)} async-done(((bf16[8,24,1,2048]{3,1,2,0:T(8,128)(2,1)}), bf16[8,24,1,2048]{3,1,2,0:T(8,128)(2,1)}, u32[]{:S(2)}, u32[]{:S(2)}) %all-to-all-start.1) | async-done | bytes 786464 | tf_op jit(solution)/shard_map/all_to_all | solution.py:72
  112.7 2.1 %gather_fusion = bf16[64,2048]{1,0:T(8,128)(2,1)} fusion(bf16[1,96,2048]{2,1,0:T(8,128)(2,1)S(1)} %bitcast.132, s32[64]{0:T(128)S(1)} %or_bitcast_fusion.1), kind=kCustom, calls=%fused_computation | custom fusion | bytes 524800 | tf_op jit(solution)/shard_map/gather | solution.py:79
  114.8 2.1 %reshape.657 = f32[1,32,2,2048]{3,2,1,0:T(2,128)} reshape(bf16[64,2048]{1,0:T(8,128)(2,1)} %gather_fusion) | data formatting | bytes 786432 | tf_op jit(solution)/shard_map/convert_element_type | solution.py:83
  116.9 1.8 %multiply_reduce_fusion = f32[32,2048]{1,0:T(8,128)S(1)} fusion(f32[1,32,2,2048]{3,2,1,0:T(2,128)} %reshape.660, f32[32,2]{1,0:T(8,128)} %copy.58), kind=kLoop, calls=%fused_computation.14 | loop fusion | flops 196608 | bytes 786688 | tf_op jit(solution)/shard_map/reduce_sum | solution.py:82
  118.7 1.8 %multiply_reduce_fusion.1 = f32[32,2048]{1,0:T(8,128)S(1)} fusion(f32[1,32,2,2048]{3,2,1,0:T(2,128)} %reshape.657, f32[32,2]{1,0:T(8,128)S(1)} %copy-done.3), kind=kLoop, calls=%fused_computation.15 | loop fusion | flops 196608 | bytes 786688 | tf_op jit(solution)/shard_map/reduce_sum | solution.py:82
  120.6 1.5 %collective-permute-start = (bf16[1,32,2048]{2,1,0:T(8,128)(2,1)S(1)}, bf16[1,32,2048]{2,1,0:T(8,128)(2,1)S(1)}, u32[]{:S(2)}, u32[]{:S(2)}) collective-permute-start(bf16[1,32,2048]{2,1,0:T(8,128)(2,1)S(1)} %get-tuple-element.7), channel_id=1, source_target_pairs={{0,8},{8,16},{16,24},{24,0},{1,9},{9,17},{17,25},{25,1},{2,10},{10... | collective-permute-start | bytes 393224 | tf_op jit(solution)/shard_map/ppermute | solution.py:12
  122.1 1.5 %collective-permute-start.1 = (bf16[1,32,2048]{2,1,0:T(8,128)(2,1)S(1)}, bf16[1,32,2048]{2,1,0:T(8,128)(2,1)S(1)}, u32[]{:S(2)}, u32[]{:S(2)}) collective-permute-start(bf16[1,32,2048]{2,1,0:T(8,128)(2,1)S(1)} %get-tuple-element.8), channel_id=1, source_target_pairs={{0,8},{8,16},{16,24},{24,0},{1,9},{9,17},{17,25},{25,1},{2,10},{10... | collective-permute-start | bytes 393224 | tf_op jit(solution)/shard_map/ppermute | solution.py:12
  123.6 4.3 %collective-permute-done = bf16[1,32,2048]{2,1,0:T(8,128)(2,1)S(1)} collective-permute-done((bf16[1,32,2048]{2,1,0:T(8,128)(2,1)S(1)}, bf16[1,32,2048]{2,1,0:T(8,128)(2,1)S(1)}, u32[]{:S(2)}, u32[]{:S(2)}) %collective-permute-start) | collective-permute-done | bytes 131104 | tf_op jit(solution)/shard_map/ppermute | solution.py:12
  127.9 1.4 %collective-permute-done.1 = bf16[1,32,2048]{2,1,0:T(8,128)(2,1)S(1)} collective-permute-done((bf16[1,32,2048]{2,1,0:T(8,128)(2,1)S(1)}, bf16[1,32,2048]{2,1,0:T(8,128)(2,1)S(1)}, u32[]{:S(2)}, u32[]{:S(2)}) %collective-permute-start.1) | collective-permute-done | bytes 131104 | tf_op jit(solution)/shard_map/ppermute | solution.py:12
  (54 shorter events, 11.4 us)
Async XLA Ops:
  0.0 40.2 %copy-start = (bf16[1,1,2048,768]{3,2,1,0:T(8,128)(2,1)S(1)}, bf16[1,1,2048,768]{3,2,1,0:T(8,128)(2,1)}, u32[]{:S(2)}) copy-start(bf16[1,1,2048,768]{3,2,1,0:T(8,128)(2,1)} %param.10) | copy-start | bytes 9437188
  4.3 8.7 %copy-start.1 = (bf16[1,2,32,2048]{3,2,1,0:T(8,128)(2,1)S(1)}, bf16[1,2,32,2048]{3,2,1,0:T(8,128)(2,1)}, u32[]{:S(2)}) copy-start(bf16[1,2,32,2048]{3,2,1,0:T(8,128)(2,1)} %param.6) | copy-start | bytes 786436
  4.3 8.7 %copy-start.4 = (f32[1,2048]{1,0:T(1,128)S(1)}, f32[1,2048]{1,0:T(1,128)}, u32[]{:S(2)}) copy-start(f32[1,2048]{1,0:T(1,128)} %param.9) | copy-start | bytes 24580
  6.6 27.4 %all-to-all-start.2 = ((bf16[8,24,1,2048]{3,1,2,0:T(8,128)(2,1)}), bf16[8,24,1,2048]{3,1,2,0:T(8,128)(2,1)}, u32[]{:S(2)}, u32[]{:S(2)}) async-start(bf16[8,24,1,2048]{3,1,2,0:T(8,128)(2,1)} %bitcast.133), calls=%async_computation.2 | async-start | bytes 1572864 | tf_op jit(solution)/shard_map/all_to_all | solution.py:70
  36.0 25.2 %all-to-all-start = ((bf16[8,24,1,2048]{3,1,2,0:T(8,128)(2,1)}), bf16[8,24,1,2048]{3,1,2,0:T(8,128)(2,1)}, u32[]{:S(2)}, u32[]{:S(2)}) async-start(bf16[8,24,1,2048]{3,1,2,0:T(8,128)(2,1)} %bitcast.134), calls=%async_computation | async-start | bytes 1572864 | tf_op jit(solution)/shard_map/all_to_all | solution.py:70
  40.2 2.1 %copy-start.6 = (bf16[1,1,384,2048]{3,2,1,0:T(8,128)(2,1)S(1)}, bf16[1,1,384,2048]{3,2,1,0:T(8,128)(2,1)}, u32[]{:S(2)}) copy-start(bf16[1,1,384,2048]{3,2,1,0:T(8,128)(2,1)} %param.11) | copy-start | bytes 4718596
  43.8 21.8 %copy-start.5 = (f32[1,2,32,2]{2,3,1,0:T(2,128)S(1)}, f32[1,2,32,2]{2,3,1,0:T(2,128)}, u32[]{:S(2)}) copy-start(f32[1,2,32,2]{2,3,1,0:T(2,128)} %param.8) | copy-start | bytes 1540
  61.2 25.2 %all-to-all-start.3 = ((bf16[8,24,1,2048]{3,1,2,0:T(8,128)(2,1)}), bf16[8,24,1,2048]{3,1,2,0:T(8,128)(2,1)}, u32[]{:S(2)}, u32[]{:S(2)}) async-start(bf16[8,24,1,2048]{3,1,2,0:T(8,128)(2,1)} %bitcast.138), calls=%async_computation.3 | async-start | bytes 1572864 | tf_op jit(solution)/shard_map/all_to_all | solution.py:72
  65.6 2.0 %copy-start.7 = (bf16[1,1,384,2048]{3,2,1,0:T(8,128)(2,1)S(1)}, bf16[1,1,384,2048]{3,2,1,0:T(8,128)(2,1)}, u32[]{:S(2)}) copy-start(bf16[1,1,384,2048]{3,2,1,0:T(8,128)(2,1)} %param.11) | copy-start | bytes 4718596
  86.3 25.2 %all-to-all-start.1 = ((bf16[8,24,1,2048]{3,1,2,0:T(8,128)(2,1)}), bf16[8,24,1,2048]{3,1,2,0:T(8,128)(2,1)}, u32[]{:S(2)}, u32[]{:S(2)}) async-start(bf16[8,24,1,2048]{3,1,2,0:T(8,128)(2,1)} %bitcast.137), calls=%async_computation.1 | async-start | bytes 1572864 | tf_op jit(solution)/shard_map/all_to_all | solution.py:72
  114.8 3.9 %copy-start.3 = (f32[32,2]{1,0:T(8,128)S(1)}, f32[32,2]{1,0:T(8,128)}, u32[]{:S(2)}) copy-start(f32[32,2]{1,0:T(8,128)} %copy.51) | copy-start | bytes 772
  114.8 5.7 %copy-start.2 = (bf16[1,2,32,2048]{3,2,1,0:T(8,128)(2,1)S(1)}, bf16[1,2,32,2048]{3,2,1,0:T(8,128)(2,1)}, u32[]{:S(2)}) copy-start(bf16[1,2,32,2048]{3,2,1,0:T(8,128)(2,1)} %param.6) | copy-start | bytes 786436
  120.6 7.3 %collective-permute-start = (bf16[1,32,2048]{2,1,0:T(8,128)(2,1)S(1)}, bf16[1,32,2048]{2,1,0:T(8,128)(2,1)S(1)}, u32[]{:S(2)}, u32[]{:S(2)}) collective-permute-start(bf16[1,32,2048]{2,1,0:T(8,128)(2,1)S(1)} %get-tuple-element.7), channel_id=1, source_target_pairs={{0,8},{8,16},{16,24},{24,0},{1,9},{9,17},{17,25},{25,1},{2,10},{10... | collective-permute-start | bytes 393224 | tf_op jit(solution)/shard_map/ppermute | solution.py:12
  122.1 7.2 %collective-permute-start.1 = (bf16[1,32,2048]{2,1,0:T(8,128)(2,1)S(1)}, bf16[1,32,2048]{2,1,0:T(8,128)(2,1)S(1)}, u32[]{:S(2)}, u32[]{:S(2)}) collective-permute-start(bf16[1,32,2048]{2,1,0:T(8,128)(2,1)S(1)} %get-tuple-element.8), channel_id=1, source_target_pairs={{0,8},{8,16},{16,24},{24,0},{1,9},{9,17},{17,25},{25,1},{2,10},{10... | collective-permute-start | bytes 393224 | tf_op jit(solution)/shard_map/ppermute | solution.py:12
where the time goes:
time: 131 us; the launch traced here: 130 us
  waiting for transfers between devices  74.1 us (57%)
  starting transfers between devices  22 us (17%)
  local copies, waits for them, and re-layouts  14 us (11%)
  other arithmetic  10.3 us (8%)
  matrix products  9.4 us (7%)
    all_to_all x2, waiting for transfers between devices, local(): lax.all_to_all(outgoing, 'expert', split_axis=0, concat_axis=0, tiled=True)  37.3 us
    all_to_all x2, waiting for transfers between devices, local(): lax.all_to_all(parts, 'expert', split_axis=0, concat_axis=0, tiled=True)  31.1 us
    all_to_all x2, starting transfers between devices, local(): lax.all_to_all(outgoing, 'expert', split_axis=0, concat_axis=0, tiled=True)  10.6 us
    all_to_all x2, starting transfers between devices, local(): lax.all_to_all(parts, 'expert', split_axis=0, concat_axis=0, tiled=True)  8.4 us
    ppermute x2, waiting for transfers between devices, from_behind(): return lax.ppermute(value, axis, pairs)  5.67 us
    gather x2, local copies, waits for them, and re-layouts, local(): table[jnp.arange(count)[:, None], flat_codes]  4.22 us
    convert_element_type x2, local copies, waits for them, and re-layouts, local(): picked.astype(jnp.float32)  4.21 us
    dot_general x2, matrix products, expert_half(): joined = jnp.dot(token_rows, weights_gu, preferred_element_type=jnp.float32)  4.06 us
  transfers between devices with their start and end apart: 6, of which 6 were waited for; matrix products, arithmetic and copies ran while one was open for 12% of the time, Pallas kernels for 0%

commit v1 on v0

v1 whole, which is shorter than its diff:
```python
import jax
import jax.numpy as jnp
from jax import lax
from jax.sharding import PartitionSpec as P

EPSILON = 1e-06


def from_behind(value, axis, steps):
    count = lax.axis_size(axis)
    pairs = [(source, (source + steps) % count) for source in range(count)]
    return lax.ppermute(value, axis, pairs)


def normalize(block, gain):
    values = block.astype(jnp.float32)
    scale = lax.rsqrt(jnp.mean(values * values, axis=-1, keepdims=True) + EPSILON)
    return (values * scale * gain).astype(jnp.bfloat16)


def expert_half(token_rows, weights_gu, weights_dn):
    units = weights_dn.shape[0]
    joined = jnp.dot(token_rows, weights_gu, preferred_element_type=jnp.float32)
    hidden = (jax.nn.silu(joined[:, :units]) * joined[:, units:]).astype(jnp.bfloat16)
    partial_out = jnp.dot(hidden, weights_dn, preferred_element_type=jnp.float32)
    return partial_out.astype(jnp.bfloat16)


def local(tokens, routes, combine_weights, norm_gain, gate_up, down):
    inputs = tokens[0]
    micro, tok_count, width = inputs.shape
    experts = lax.axis_size("expert") // 2
    mine = lax.axis_index("expert") // 2
    normed = normalize(inputs, norm_gain[0])
    names = jnp.arange(experts, dtype=routes.dtype)
    chosen = routes[0][..., None] == names
    table = jnp.sum(jnp.where(chosen, combine_weights[0][..., None], 0.0), axis=2)
    every = lax.all_gather(normed, "expert", axis=1, tiled=True)
    tables = lax.all_gather(table, "expert", axis=1, tiled=True)
    weights = jnp.sum(jnp.where(names == mine, tables, 0.0), axis=-1)
    rows = every.reshape(-1, width)
    partial_out = expert_half(rows, gate_up[0, 0], down[0, 0])
    scaled = weights.reshape(-1, 1) * partial_out.astype(jnp.float32)
    scaled = scaled.astype(jnp.bfloat16).reshape(micro, -1, width)
    summed = lax.psum_scatter(scaled, "expert", scatter_dimension=1, tiled=True)
    mixed = inputs.astype(jnp.float32) + summed.astype(jnp.float32)
    moved = from_behind(mixed.astype(jnp.bfloat16), "section", 1)
    return moved[None]


def solution(mesh):
    return jax.shard_map(
        local,
        mesh=mesh,
        in_specs=(
            P("section", None, "expert", None),
            P("section", None, "expert", None),
            P("section", None, "expert", None),
            P("section", None),
            P("section", "expert", None, None),
            P("section", "expert", None, None),
        ),
        out_specs=P("section", None, "expert", None),
        check_vma=False,
    )
```

time: 131 us -> 100 us (0.76)
  starting transfers between devices: 22 us -> 1.61 us
  waiting for transfers between devices: 74.1 us -> 56.4 us
  blocking collectives: 0 us -> 16.2 us
  between operations: 0.28 us -> 13.4 us
  local copies, waits for them, and re-layouts: 14 us -> 0.9 us
  other arithmetic: 10.3 us -> 5.11 us
  matrix products: 9.4 us -> 6.12 us
    all_to_all x4 -> x0, waiting for transfers between devices: 68.4 us -> none  [the longest x2 37.3 us: local(): lax.all_to_all(outgoing, 'expert', split_axis=0, concat_axis=0, tiled=True)]
    reduce_scatter x0 -> x1, waiting for transfers between devices: none -> 35.4 us  [local(): summed = lax.psum_scatter(scaled, 'expert', scatter_dimension=1, tiled=True)]
    all_to_all x4 -> x0, starting transfers between devices: 19 us -> none  [the longest x2 10.6 us: local(): lax.all_to_all(outgoing, 'expert', split_axis=0, concat_axis=0, tiled=True)]
    all_gather x0 -> x1, blocking collectives: none -> 16.2 us  [local(): tables = lax.all_gather(table, 'expert', axis=1, tiled=True)]
    all_gather x0 -> x1, waiting for transfers between devices: none -> 15.2 us  [local(): every = lax.all_gather(normed, 'expert', axis=1, tiled=True)]
    gather x2 -> x0, local copies, waits for them, and re-layouts: 4.22 us -> none  [local(): table[jnp.arange(count)[:, None], flat_codes]]
    convert_element_type x2 -> x0, local copies, waits for them, and re-layouts: 4.21 us -> none  [local(): picked.astype(jnp.float32)]
    broadcast_in_dim x2 -> x0, local copies, waits for them, and re-layouts: 2.97 us -> none  [local(): outgoing = jnp.repeat(buffer, 2, axis=0)]
  transfers between devices with their start and end apart: 6 -> 3, of which waited for: 6 -> 3; matrix products, arithmetic and copies ran while one was open for 12% -> 1% of each run, Pallas kernels for 0% -> 0%
where the time goes in v1:
time: 100 us; the launch traced here: 99.7 us
  waiting for transfers between devices  56.4 us (56%)
  blocking collectives  16.2 us (16%)
  between operations  13.4 us (13%)
  matrix products  6.12 us (6%)
  other arithmetic  5.11 us (5%)
  starting transfers between devices  1.61 us (2%)
    reduce_scatter x1, waiting for transfers between devices, local(): summed = lax.psum_scatter(scaled, 'expert', scatter_dimension=1, tiled=True)  35.4 us
    all_gather x1, blocking collectives, local(): tables = lax.all_gather(table, 'expert', axis=1, tiled=True)  16.2 us
    all_gather x1, waiting for transfers between devices, local(): every = lax.all_gather(normed, 'expert', axis=1, tiled=True)  15.2 us
    ppermute x1, waiting for transfers between devices, from_behind(): return lax.ppermute(value, axis, pairs)  5.76 us
    dot_general x1, matrix products, expert_half(): joined = jnp.dot(token_rows, weights_gu, preferred_element_type=jnp.float32)  3.49 us
    dot_general x1, matrix products, expert_half(): jnp.dot(hidden, weights_dn, preferred_element_type=jnp.float32)  2.63 us
  transfers between devices with their start and end apart: 3, of which 3 were waited for; matrix products, arithmetic and copies ran while one was open for 1% of the time, Pallas kernels for 0%

profile of v1, /device:TPU:0, one launch (start us, length us, event | category | flops | bytes accessed | tf_op | source)
XLA Modules:
  0.0 99.7 jit_solution(1353674424662216050)
XLA Ops:
  6.5 0.0 copy-start
  6.5 0.0 all-gather.2.cloned.1.call-start
  6.5 1.2 %fusion.4 = f32[2,32]{1,0:T(2,128)S(1)} fusion(bf16[1,2,32,2048]{3,2,1,0:T(8,128)(2,1)} %param.6), kind=kLoop, calls=%fused_computation.10 | loop fusion | flops 393152 | bytes 262400 | tf_op jit(solution)/shard_map/reduce_sum | solution.py:17
  7.8 1.8 %fusion.6 = bf16[2,32,2048]{2,1,0:T(8,128)(2,1)} fusion(bf16[1,2,32,2048]{3,2,1,0:T(8,128)(2,1)} %param.6, f32[2048]{0:T(1024)} %bitcast.22, f32[2,32]{1,0:T(2,128)S(1)} %add_rsqrt_fusion), kind=kLoop, calls=%fused_computation.12 | loop fusion | flops 524288 | bytes 532736 | tf_op jit(solution)/shard_map/convert_element_type | solution.py:18
  9.6 0.0 all-gather.2.cloned.1.call-update
  9.6 0.0 reduce-scatter.2.cloned.1.call-start
  9.7 0.7 select_reduce_fusion.1
  10.4 0.1 copy.9
  10.5 16.2 %all_gather.6 = f32[2,256,4]{2,0,1:T(2,128)S(1)} all-gather(f32[2,32,4]{2,0,1:T(2,128)S(1)} %copy.9), channel_id=1, replica_groups=mesh['section'=4,'expert'=8] {'expert'}, dimensions={1}, use_global_device_ids=true | all-gather | bytes 9216 | tf_op jit(solution)/shard_map/all_gather | solution.py:39
  26.7 0.3 select_reduce_fusion
  27.0 0.1 copy.11
  27.1 15.2 %all-gather.2.cloned.1.call-done = bf16[2,256,2048]{2,1,0:T(8,128)(2,1)} async-done(((bf16[2,32,2048]{2,1,0:T(8,128)(2,1)}), bf16[2,256,2048]{2,1,0:T(8,128)(2,1)}) %all-gather.2.cloned.1.call-update) | async-done | bytes 2097168 | tf_op jit(solution)/shard_map/all_gather | solution.py:38
  42.3 0.0 copy-done
  42.3 0.0 copy-start.2
  42.3 3.5 %fusion = f32[512,768]{1,0:T(8,128)S(1)} fusion(bf16[512,2048]{1,0:T(8,128)(2,1)} %bitcast.27, bf16[1,1,2048,768]{3,2,1,0:T(8,128)(2,1)S(1)} %copy-done), kind=kOutput, calls=%fused_computation.1 | convolution fusion | flops 1610612736 | bytes 6815744 | tf_op jit(solution)/shard_map/dot_general | solution.py:23
  45.8 0.0 copy-done.2
  45.8 2.6 %multiply_convert_fusion = bf16[512,2048]{1,0:T(8,128)(2,1)} fusion(f32[512]{0:T(512)S(1)} %bitcast.24, bf16[1,1,384,2048]{3,2,1,0:T(8,128)(2,1)S(1)} %copy-done.2, f32[512,768]{1,0:T(8,128)S(1)} %fusion), kind=kOutput, calls=%fused_computation | convolution fusion | flops 810680320 | bytes 5244928 | tf_op jit(solution)/shard_map/dot_general | solution.py:25
  48.4 0.0 reduce-scatter.2.cloned.1.call-update
  48.5 35.4 %reduce-scatter.2.cloned.1.call-done = bf16[2,32,2048]{2,1,0:T(8,128)(2,1)} async-done(((bf16[2,256,2048]{2,1,0:T(8,128)(2,1)}), bf16[2,32,2048]{2,1,0:T(8,128)(2,1)}) %reduce-scatter.2.cloned.1.call-update) | async-done | bytes 262160 | tf_op jit(solution)/shard_map/reduce_scatter | solution.py:45
  83.9 0.0 copy-done.1
  83.9 1.0 %fusion.7 = bf16[2,32,2048]{2,1,0:T(8,128)(2,1)S(1)} fusion(bf16[2,32,2048]{2,1,0:T(8,128)(2,1)} %reduce-scatter.2.cloned.1.call-done, bf16[1,2,32,2048]{3,2,1,0:T(8,128)(2,1)S(1)} %copy-done.1), kind=kLoop, calls=%fused_computation.13 | loop fusion | flops 524288 | bytes 786432 | tf_op jit(solution)/shard_map/convert_element_type | solution.py:47
  84.9 1.6 %collective-permute-start = (bf16[2,32,2048]{2,1,0:T(8,128)(2,1)S(1)}, bf16[2,32,2048]{2,1,0:T(8,128)(2,1)S(1)}, u32[]{:S(2)}, u32[]{:S(2)}) collective-permute-start(bf16[2,32,2048]{2,1,0:T(8,128)(2,1)S(1)} %fusion.7), channel_id=1, source_target_pairs={{0,8},{8,16},{16,24},{24,0},{1,9},{9,17},{17,25},{25,1},{2,10},{10... | collective-permute-start | bytes 786440 | tf_op jit(solution)/shard_map/ppermute | solution.py:12
  86.4 5.8 %collective-permute-done = bf16[2,32,2048]{2,1,0:T(8,128)(2,1)S(1)} collective-permute-done((bf16[2,32,2048]{2,1,0:T(8,128)(2,1)S(1)}, bf16[2,32,2048]{2,1,0:T(8,128)(2,1)S(1)}, u32[]{:S(2)}, u32[]{:S(2)}) %collective-permute-start) | collective-permute-done | bytes 262176 | tf_op jit(solution)/shard_map/ppermute | solution.py:12
  92.2 0.7 copy.14
  (4 shorter events, 0.0 us)
Async XLA Ops:
  6.5 35.8 %copy-start = (bf16[1,1,2048,768]{3,2,1,0:T(8,128)(2,1)S(1)}, bf16[1,1,2048,768]{3,2,1,0:T(8,128)(2,1)}, u32[]{:S(2)}) copy-start(bf16[1,1,2048,768]{3,2,1,0:T(8,128)(2,1)} %param.10) | copy-start | bytes 9437188
  6.5 35.7 %all-gather.2.cloned.1.call-start = ((), (), s32[]{:S(2)}) async-start(), calls=%async_computation.1 | async-start | bytes 2359296 | tf_op jit(solution)/shard_map/all_gather | solution.py:38
  9.6 74.3 %reduce-scatter.2.cloned.1.call-start = ((), (), s32[]{:S(2)}) async-start(), calls=%async_computation.2 | async-start | bytes 2359296 | tf_op jit(solution)/shard_map/reduce_scatter | solution.py:45
  42.3 3.5 %copy-start.2 = (bf16[1,1,384,2048]{3,2,1,0:T(8,128)(2,1)S(1)}, bf16[1,1,384,2048]{3,2,1,0:T(8,128)(2,1)}, u32[]{:S(2)}) copy-start(bf16[1,1,384,2048]{3,2,1,0:T(8,128)(2,1)} %param.11) | copy-start | bytes 4718596
  48.4 35.4 %copy-start.1 = (bf16[1,2,32,2048]{3,2,1,0:T(8,128)(2,1)S(1)}, bf16[1,2,32,2048]{3,2,1,0:T(8,128)(2,1)}, u32[]{:S(2)}) copy-start(bf16[1,2,32,2048]{3,2,1,0:T(8,128)(2,1)} %param.6) | copy-start | bytes 786436
  84.9 7.3 %collective-permute-start = (bf16[2,32,2048]{2,1,0:T(8,128)(2,1)S(1)}, bf16[2,32,2048]{2,1,0:T(8,128)(2,1)S(1)}, u32[]{:S(2)}, u32[]{:S(2)}) collective-permute-start(bf16[2,32,2048]{2,1,0:T(8,128)(2,1)S(1)} %fusion.7), channel_id=1, source_target_pairs={{0,8},{8,16},{16,24},{24,0},{1,9},{9,17},{17,25},{25,1},{2,10},{10... | collective-permute-start | bytes 786440 | tf_op jit(solution)/shard_map/ppermute | solution.py:12
Sparse Core Ops, SparseCore 0:
  9.7 32.5 all-gather.1
  48.6 35.2 reduce-scatter.1

commit v2 on v1

--- a/solution.py
+++ b/solution.py
@@ -35,10 +35,15 @@
     names = jnp.arange(experts, dtype=routes.dtype)
     chosen = routes[0][..., None] == names
     table = jnp.sum(jnp.where(chosen, combine_weights[0][..., None], 0.0), axis=2)
-    every = lax.all_gather(normed, "expert", axis=1, tiled=True)
-    tables = lax.all_gather(table, "expert", axis=1, tiled=True)
+    high = table.astype(jnp.bfloat16)
+    low = (table - high.astype(jnp.float32)).astype(jnp.bfloat16)
+    spare = jnp.zeros((micro, tok_count, 128 - 2 * experts), jnp.bfloat16)
+    packed = jnp.concatenate([normed, high, low, spare], axis=-1)
+    every = lax.all_gather(packed, "expert", axis=1, tiled=True)
+    tables = every[..., width : width + experts].astype(jnp.float32)
+    tables = tables + every[..., width + experts : width + 2 * experts].astype(jnp.float32)
     weights = jnp.sum(jnp.where(names == mine, tables, 0.0), axis=-1)
-    rows = every.reshape(-1, width)
+    rows = every[..., :width].reshape(-1, width)
     partial_out = expert_half(rows, gate_up[0, 0], down[0, 0])
     scaled = weights.reshape(-1, 1) * partial_out.astype(jnp.float32)
     scaled = scaled.astype(jnp.bfloat16).reshape(micro, -1, width)

time: 100 us -> 103 us (1.030)
  waiting for transfers between devices: 56.4 us -> 74.3 us
  blocking collectives: 16.2 us -> 0 us
  local copies, waits for them, and re-layouts: 0.9 us -> 3.32 us
  matrix products: 6.12 us -> 4.46 us
    all_gather x1, waiting for transfers between devices: 15.2 us -> 33 us  [local(): every = lax.all_gather(packed, 'expert', axis=1, tiled=True)]
    all_gather x1 -> x0, blocking collectives: 16.2 us -> none  [local(): tables = lax.all_gather(table, 'expert', axis=1, tiled=True)]
    dot_general x1, matrix products: 3.49 us -> 1.81 us  [expert_half(): joined = jnp.dot(token_rows, weights_gu, preferred_element_type=jnp.float32)]
    slice x0 -> x2, local copies, waits for them, and re-layouts: none -> 1.58 us  [local(): rows = every[..., :width].reshape(-1, width)]
  transfers between devices with their start and end apart: 3 -> 3, of which waited for: 3 -> 3; matrix products, arithmetic and copies ran while one was open for 1% -> 0% of each run, Pallas kernels for 0% -> 0%
where the time goes in v2:
time: 103 us; the launch traced here: 102 us
  waiting for transfers between devices  74.3 us (72%)
  between operations  13.5 us (13%)
  other arithmetic  5.28 us (5%)
  matrix products  4.46 us (4%)
  local copies, waits for them, and re-layouts  3.32 us (3%)
  starting transfers between devices  1.56 us (2%)
    reduce_scatter x1, waiting for transfers between devices, local(): summed = lax.psum_scatter(scaled, 'expert', scatter_dimension=1, tiled=True)  35.4 us
    all_gather x1, waiting for transfers between devices, local(): every = lax.all_gather(packed, 'expert', axis=1, tiled=True)  33 us
    ppermute x1, waiting for transfers between devices, from_behind(): return lax.ppermute(value, axis, pairs)  5.81 us
    dot_general x1, matrix products, expert_half(): jnp.dot(hidden, weights_dn, preferred_element_type=jnp.float32)  2.66 us
  transfers between devices with their start and end apart: 3, of which 3 were waited for; matrix products, arithmetic and copies ran while one was open for 0% of the time, Pallas kernels for 0%

profile of v2, /device:TPU:0, one launch (start us, length us, event | category | flops | bytes accessed | tf_op | source)
XLA Modules:
  0.0 102.4 jit_solution(13451900504737968637)
XLA Ops:
  6.5 0.0 copy-start
  6.5 0.0 all-gather.2.cloned.1.call-start
  6.5 1.2 %fusion.4 = f32[2,32]{1,0:T(2,128)S(1)} fusion(bf16[1,2,32,2048]{3,2,1,0:T(8,128)(2,1)} %param.6), kind=kLoop, calls=%fused_computation.10 | loop fusion | flops 393152 | bytes 262400 | tf_op jit(solution)/shard_map/reduce_sum | solution.py:17
  7.8 0.7 select_reduce_fusion.1
  8.5 0.1 copy.10
  8.6 0.1 copy.9
  8.7 1.1 %fusion.6 = bf16[2,32,2048]{2,1,0:T(8,128)(2,1)S(1)} fusion(bf16[1,2,32,2048]{3,2,1,0:T(8,128)(2,1)} %param.6, f32[2048]{0:T(1024)} %bitcast.23, f32[2,32]{1,0:T(2,128)S(1)} %add_rsqrt_fusion), kind=kLoop, calls=%fused_computation.12 | loop fusion | flops 524288 | bytes 532736 | tf_op jit(solution)/shard_map/convert_element_type | solution.py:18
  9.8 0.8 concatenate.3
  10.6 0.0 all-gather.2.cloned.1.call-update
  10.7 0.0 reduce-scatter.2.cloned.1.call-start
  10.7 33.0 %all-gather.2.cloned.1.call-done = bf16[2,256,2176]{2,1,0:T(8,128)(2,1)} async-done(((bf16[2,32,2176]{2,1,0:T(8,128)(2,1)}), bf16[2,256,2176]{2,1,0:T(8,128)(2,1)}) %all-gather.2.cloned.1.call-update) | async-done | bytes 2228240 | tf_op jit(solution)/shard_map/all_gather | solution.py:42
  43.8 1.2 %select_reduce_fusion = f32[2,256]{1,0:T(2,128)S(1)} fusion(bf16[2,256,2176]{2,1,0:T(8,128)(2,1)} %all-gather.2.cloned.1.call-done, pred[4]{0:T(512)(128)(4,1)S(1)} %iota_compare_fusion.1), kind=kLoop, calls=%fused_computation.15 | loop fusion | flops 9728 | bytes 10244 | tf_op jit(solution)/shard_map/reduce_sum | solution.py:45
  45.0 0.0 slice-start
  45.0 0.0 copy-done
  45.0 1.6 %slice-done = bf16[2,256,2048]{2,1,0:T(8,128)(2,1)S(1)} async-done(((bf16[2,256,2176]{2,1,0:T(8,128)(2,1)}), bf16[2,256,2048]{2,1,0:T(8,128)(2,1)S(1)}, s32[]{:S(2)}) %slice-start) | async-done | bytes 2097176 | tf_op jit(solution)/shard_map/slice | solution.py:46
  46.6 1.8 %fusion = f32[512,768]{1,0:T(8,128)S(1)} fusion(bf16[512,2048]{1,0:T(8,128)(2,1)S(1)} %bitcast.20, bf16[1,1,2048,768]{3,2,1,0:T(8,128)(2,1)S(1)} %copy-done), kind=kOutput, calls=%fused_computation.1 | convolution fusion | flops 1610612736 | bytes 6815744 | tf_op jit(solution)/shard_map/dot_general | solution.py:23
  48.4 2.7 %multiply_convert_fusion = bf16[512,2048]{1,0:T(8,128)(2,1)} fusion(f32[512]{0:T(512)S(1)} %bitcast.25, bf16[1,1,384,2048]{3,2,1,0:T(8,128)(2,1)S(1)} %copy-done.2, f32[512,768]{1,0:T(8,128)S(1)} %fusion), kind=kOutput, calls=%fused_computation | convolution fusion | flops 810680320 | bytes 5244928 | tf_op jit(solution)/shard_map/dot_general | solution.py:25
  51.1 0.0 reduce-scatter.2.cloned.1.call-update
  51.1 35.4 %reduce-scatter.2.cloned.1.call-done = bf16[2,32,2048]{2,1,0:T(8,128)(2,1)} async-done(((bf16[2,256,2048]{2,1,0:T(8,128)(2,1)}), bf16[2,32,2048]{2,1,0:T(8,128)(2,1)}) %reduce-scatter.2.cloned.1.call-update) | async-done | bytes 262160 | tf_op jit(solution)/shard_map/reduce_scatter | solution.py:50
  86.5 0.0 copy-done.1
  86.5 1.0 fusion.7
  87.5 1.5 %collective-permute-start = (bf16[2,32,2048]{2,1,0:T(8,128)(2,1)S(1)}, bf16[2,32,2048]{2,1,0:T(8,128)(2,1)S(1)}, u32[]{:S(2)}, u32[]{:S(2)}) collective-permute-start(bf16[2,32,2048]{2,1,0:T(8,128)(2,1)S(1)} %fusion.7), channel_id=1, source_target_pairs={{0,8},{8,16},{16,24},{24,0},{1,9},{9,17},{17,25},{25,1},{2,10},{10... | collective-permute-start | bytes 786440 | tf_op jit(solution)/shard_map/ppermute | solution.py:12
  89.0 5.8 %collective-permute-done = bf16[2,32,2048]{2,1,0:T(8,128)(2,1)S(1)} collective-permute-done((bf16[2,32,2048]{2,1,0:T(8,128)(2,1)S(1)}, bf16[2,32,2048]{2,1,0:T(8,128)(2,1)S(1)}, u32[]{:S(2)}, u32[]{:S(2)}) %collective-permute-start) | collective-permute-done | bytes 262176 | tf_op jit(solution)/shard_map/ppermute | solution.py:12
  94.8 0.7 copy.13
  (8 shorter events, 0.0 us)
Async XLA Ops:
  6.5 38.5 %copy-start = (bf16[1,1,2048,768]{3,2,1,0:T(8,128)(2,1)S(1)}, bf16[1,1,2048,768]{3,2,1,0:T(8,128)(2,1)}, u32[]{:S(2)}) copy-start(bf16[1,1,2048,768]{3,2,1,0:T(8,128)(2,1)} %param.10) | copy-start | bytes 9437188
  6.5 37.2 %all-gather.2.cloned.1.call-start = ((), (), s32[]{:S(2)}) async-start(), calls=%async_computation.1 | async-start | bytes 2506752 | tf_op jit(solution)/shard_map/all_gather | solution.py:42
  10.7 75.8 %reduce-scatter.2.cloned.1.call-start = ((), (), s32[]{:S(2)}) async-start(), calls=%async_computation.2 | async-start | bytes 2359296 | tf_op jit(solution)/shard_map/reduce_scatter | solution.py:50
  45.0 1.6 %slice-start = ((bf16[2,256,2176]{2,1,0:T(8,128)(2,1)}), bf16[2,256,2048]{2,1,0:T(8,128)(2,1)S(1)}, s32[]{:S(2)}) async-start(bf16[2,256,2176]{2,1,0:T(8,128)(2,1)} %all-gather.2.cloned.1.call-done), calls=%async_computation.3 | async-start | bytes 4194304 | tf_op jit(solution)/shard_map/slice | solution.py:46
  46.6 1.8 %copy-start.2 = (bf16[1,1,384,2048]{3,2,1,0:T(8,128)(2,1)S(1)}, bf16[1,1,384,2048]{3,2,1,0:T(8,128)(2,1)}, u32[]{:S(2)}) copy-start(bf16[1,1,384,2048]{3,2,1,0:T(8,128)(2,1)} %param.11) | copy-start | bytes 4718596
  51.1 35.4 %copy-start.1 = (bf16[1,2,32,2048]{3,2,1,0:T(8,128)(2,1)S(1)}, bf16[1,2,32,2048]{3,2,1,0:T(8,128)(2,1)}, u32[]{:S(2)}) copy-start(bf16[1,2,32,2048]{3,2,1,0:T(8,128)(2,1)} %param.6) | copy-start | bytes 786436
  87.5 7.3 %collective-permute-start = (bf16[2,32,2048]{2,1,0:T(8,128)(2,1)S(1)}, bf16[2,32,2048]{2,1,0:T(8,128)(2,1)S(1)}, u32[]{:S(2)}, u32[]{:S(2)}) collective-permute-start(bf16[2,32,2048]{2,1,0:T(8,128)(2,1)S(1)} %fusion.7), channel_id=1, source_target_pairs={{0,8},{8,16},{16,24},{24,0},{1,9},{9,17},{17,25},{25,1},{2,10},{10... | collective-permute-start | bytes 786440 | tf_op jit(solution)/shard_map/ppermute | solution.py:12
Sparse Core Ops, SparseCore 0:
  10.8 32.9 all-gather.1
  51.2 35.2 reduce-scatter.1

commit v3 on v1

v3 whole, which is shorter than its diff:
```python
import jax
import jax.numpy as jnp
from jax import lax
from jax.sharding import Mesh
from jax.sharding import PartitionSpec as P

EPSILON = 1e-06


def from_behind(value, axis, steps):
    count = lax.axis_size(axis)
    pairs = [(source, (source + steps) % count) for source in range(count)]
    return lax.ppermute(value, axis, pairs)


def swap_cores(value):
    return lax.ppermute(value, "core", [(0, 1), (1, 0)])


def slot_codes(route_block, experts, capacity):
    flat = route_block.reshape(-1)
    onehot = (flat[:, None] == jnp.arange(experts, dtype=jnp.int32)[None, :]).astype(jnp.int32)
    before = jnp.cumsum(onehot, axis=0) - onehot
    slot = jnp.sum(before * onehot, axis=1)
    return (flat * capacity + slot).reshape(route_block.shape)


def normalize(block, gain):
    values = block.astype(jnp.float32)
    scale = lax.rsqrt(jnp.mean(values * values, axis=-1, keepdims=True) + EPSILON)
    return (values * scale * gain).astype(jnp.bfloat16)


def expert_half(token_rows, weights_gu, weights_dn):
    units = weights_dn.shape[0]
    joined = jnp.dot(token_rows, weights_gu, preferred_element_type=jnp.float32)
    hidden = (jax.nn.silu(joined[:, :units]) * joined[:, units:]).astype(jnp.bfloat16)
    partial_out = jnp.dot(hidden, weights_dn, preferred_element_type=jnp.float32)
    return partial_out.astype(jnp.bfloat16)


def local(tokens, routes, combine_weights, norm_gain, gate_up, down):
    inputs = tokens[0]
    micro, tok_count, width = inputs.shape
    experts = lax.axis_size("z")
    topk = routes.shape[3]
    capacity = 2 * ((3 * tok_count * topk + 4 * experts - 1) // (4 * experts))
    normed = normalize(inputs, norm_gain[0])
    codes = jax.vmap(lambda block: slot_codes(block, experts, capacity))(routes[0])
    lanes = jnp.arange(experts * capacity, dtype=jnp.int32)
    onehot = jnp.any(codes[..., None] == lanes, axis=2).astype(jnp.bfloat16)
    buffer = jnp.einsum("mtq,mtd->qmd", onehot, normed, preferred_element_type=jnp.float32)
    buffer = buffer.astype(jnp.bfloat16).reshape(experts, capacity, micro, width)
    incoming = lax.all_to_all(buffer, "z", split_axis=0, concat_axis=0, tiled=True)
    rows = jnp.stack([incoming, swap_cores(incoming)]).reshape(-1, width)
    parts = expert_half(rows, gate_up[0, 0], down[0, 0])
    parts = parts.reshape((2,) + incoming.shape)
    other_half = swap_cores(parts[1])
    results = (parts[0].astype(jnp.float32) + other_half.astype(jnp.float32)).astype(jnp.bfloat16)
    returned = lax.all_to_all(results, "z", split_axis=0, concat_axis=0, tiled=True)
    table = jnp.swapaxes(returned.reshape(experts * capacity, micro, width), 0, 1)
    flat_codes = codes.reshape(micro, tok_count * topk)
    picked = table[jnp.arange(micro)[:, None], flat_codes].reshape(micro, tok_count, topk, width)
    mixed = inputs.astype(jnp.float32) + jnp.sum(
        combine_weights[0][..., None] * picked.astype(jnp.float32), axis=2
    )
    moved = from_behind(mixed.astype(jnp.bfloat16), "section", 1)
    return moved[None]


def solution(mesh):
    sections, spread = mesh.devices.shape
    chips = Mesh(mesh.devices.reshape(sections, spread // 2, 2), ("section", "z", "core"))
    split = ("z", "core")
    return jax.shard_map(
        local,
        mesh=chips,
        in_specs=(
            P("section", None, split, None),
            P("section", None, split, None),
            P("section", None, split, None),
            P("section", None),
            P("section", split, None, None),
            P("section", split, None, None),
        ),
        out_specs=P("section", None, split, None),
        check_vma=False,
    )
```

time: 100 us -> 103 us (1.030)
  waiting for transfers between devices: 56.4 us -> 29.8 us
  local copies, waits for them, and re-layouts: 0.9 us -> 21.3 us
  between operations: 13.4 us -> 0.13 us
  blocking collectives: 16.2 us -> 26.3 us
  other arithmetic: 5.11 us -> 13.5 us
  starting transfers between devices: 1.61 us -> 6.2 us
    reduce_scatter x1 -> x0, waiting for transfers between devices: 35.4 us -> none  [local(): summed = lax.psum_scatter(scaled, 'expert', scatter_dimension=1, tiled=True)]
    all_to_all x0 -> x1, blocking collectives: none -> 26.3 us  [local(): lax.all_to_all(buffer, 'z', split_axis=0, concat_axis=0, tiled=True)]
    all_to_all x0 -> x1, waiting for transfers between devices: none -> 20.4 us  [local(): lax.all_to_all(results, 'z', split_axis=0, concat_axis=0, tiled=True)]
    all_gather x1 -> x0, blocking collectives: 16.2 us -> none  [local(): tables = lax.all_gather(table, 'expert', axis=1, tiled=True)]
    all_gather x1 -> x0, waiting for transfers between devices: 15.2 us -> none  [local(): every = lax.all_gather(normed, 'expert', axis=1, tiled=True)]
    convert_element_type x0 -> x2, local copies, waits for them, and re-layouts: none -> 5.75 us  [the longest x1 3.02 us: local(): parts[0].astype(jnp.float32) + other_half.astype(jnp.float32)]
    all_to_all x0 -> x1, starting transfers between devices: none -> 4.5 us  [local(): lax.all_to_all(results, 'z', split_axis=0, concat_axis=0, tiled=True)]
    reshape x0 -> x2, local copies, waits for them, and re-layouts: none -> 4.46 us  [the longest x1 3.65 us: local(): rows = jnp.stack([incoming, swap_cores(incoming)]).reshape(-1, width)]
  transfers between devices with their start and end apart: 3 -> 4, of which waited for: 3 -> 3; matrix products, arithmetic and copies ran while one was open for 1% -> 3% of each run, Pallas kernels for 0% -> 0%
where the time goes in v3:
time: 103 us; the launch traced here: 102 us
  waiting for transfers between devices  29.8 us (29%)
  blocking collectives  26.3 us (26%)
  local copies, waits for them, and re-layouts  21.3 us (21%)
  other arithmetic  13.5 us (13%)
  starting transfers between devices  6.2 us (6%)
  matrix products  5.3 us (5%)
    all_to_all x1, blocking collectives, local(): lax.all_to_all(buffer, 'z', split_axis=0, concat_axis=0, tiled=True)  26.3 us
    all_to_all x1, waiting for transfers between devices, local(): lax.all_to_all(results, 'z', split_axis=0, concat_axis=0, tiled=True)  20.4 us
    ppermute x1, waiting for transfers between devices, from_behind(): return lax.ppermute(value, axis, pairs)  7.12 us
    all_to_all x1, starting transfers between devices, local(): lax.all_to_all(results, 'z', split_axis=0, concat_axis=0, tiled=True)  4.5 us
    gather x1, local copies, waits for them, and re-layouts, local(): table[jnp.arange(micro)[:, None], flat_codes]  3.65 us
    reshape x1, local copies, waits for them, and re-layouts, local(): rows = jnp.stack([incoming, swap_cores(incoming)]).reshape(-1, width)  3.65 us
    another operation x1, other arithmetic, local(): rows = jnp.stack([incoming, swap_cores(incoming)]).reshape(-1, width)  3.44 us
    convert_element_type x1, other arithmetic, local(): (parts[0].astype(jnp.float32) + other_half.astype(jnp.float32)).astype(jn...  3.34 us
  transfers between devices with their start and end apart: 4, of which 3 were waited for; matrix products, arithmetic and copies ran while one was open for 3% of the time, Pallas kernels for 0%

profile of v3, /device:TPU:0, one launch (start us, length us, event | category | flops | bytes accessed | tf_op | source)
XLA Modules:
  0.0 102.5 jit_solution(7862642928514351914)
XLA Ops:
  0.0 0.9 copy.21
  1.6 0.7 bitcast_add_fusion
  2.4 1.1 %fusion.4 = f32[2,32]{1,0:T(2,128)S(1)} fusion(bf16[1,2,32,2048]{3,2,1,0:T(8,128)(2,1)} %param.6), kind=kLoop, calls=%fused_computation.15 | loop fusion | flops 393152 | bytes 262400 | tf_op jit(solution)/shard_map/reduce_sum | solution.py:30
  3.5 1.4 %convolution_convert_fusion.1 = bf16[2,2048,96]{1,2,0:T(8,128)(2,1)S(1)} fusion(pred[2,32,96]{2,1,0:T(8,128)(4,1)S(1)} %fusion.15, bf16[1,2,32,2048]{3,2,1,0:T(8,128)(2,1)} %param.6, f32[2048]{0:T(1024)} %bitcast.44, f32[2,32]{1,0:T(2,128)S(1)} %add_rsqrt_fusion), kind=kOutput, calls=%fused_computation.4 | convolution fusion | flops 26083328 | bytes 1063168 | tf_op jit(solution)/shard_map/mtq,mtd->qmd/dot_general | solution.py:52
  4.9 0.8 copy.23
  5.7 26.3 %all_to_all.10 = bf16[4,24,2,2048]{3,2,1,0:T(2,128)(2,1)S(1)} all-to-all(bf16[4,24,2,2048]{3,2,1,0:T(2,128)(2,1)S(1)} %copy.23), channel_id=1, replica_groups=mesh['section'=4,'z'=4,'core'=2] {'z'}, dimensions={0} | all-to-all | bytes 1572864 | tf_op jit(solution)/shard_map/all_to_all | solution.py:54
  32.0 2.3 %collective-permute-done = bf16[4,24,2,2048]{3,2,1,0:T(2,128)(2,1)S(1)} collective-permute-done((bf16[4,24,2,2048]{3,2,1,0:T(2,128)(2,1)S(1)}, bf16[4,24,2,2048]{3,2,1,0:T(2,128)(2,1)S(1)}, u32[]{:S(2)}, u32[]{:S(2)}) %collective-permute-start) | collective-permute-done | bytes 786464 | tf_op jit(solution)/shard_map/ppermute | solution.py:17
  34.3 3.4 %pad_maximum_fusion = bf16[2,4,24,2,2048]{4,3,2,1,0:T(2,128)(2,1)} fusion(bf16[1,4,24,2,2048]{4,3,2,1,0:T(2,128)(2,1)S(1)} %bitcast.42, bf16[1,4,24,2,2048]{4,3,2,1,0:T(2,128)(2,1)S(1)} %bitcast.41), kind=kLoop, calls=%fused_computation.5 | loop fusion | flops 786432 | bytes 3145728 | tf_op jit(solution)/shard_map/stack | solution.py:55
  37.7 3.6 %reshape.76 = bf16[384,2048]{1,0:T(8,128)(2,1)} reshape(bf16[2,4,24,2,2048]{4,3,2,1,0:T(2,128)(2,1)} %pad_maximum_fusion) | data formatting | bytes 3145728 | tf_op jit(solution)/shard_map/reshape | solution.py:55
  41.3 2.9 %fusion = f32[384,768]{1,0:T(8,128)S(1)} fusion(bf16[384,2048]{1,0:T(8,128)(2,1)} %reshape.76, bf16[1,1,2048,768]{3,2,1,0:T(8,128)(2,1)S(1)} %copy-done), kind=kOutput, calls=%fused_computation.1 | convolution fusion | flops 1207959552 | bytes 5898240 | tf_op jit(solution)/shard_map/dot_general | solution.py:36
  44.3 1.0 convolution_convert_fusion
  45.3 1.6 %fusion.20 = (bf16[192,2048]{1,0:T(8,128)(2,1)}, f32[192,2048]{1,0:T(8,128)}) fusion(bf16[384,2048]{1,0:T(8,128)(2,1)S(1)} %convolution_convert_fusion), kind=kLoop, calls=%fused_computation.37 | loop fusion | flops 393216 | bytes 3932160 | tf_op jit(solution)/shard_map/slice | solution.py:58
  46.9 2.8 %squeeze.13 = bf16[4,24,2,2048]{3,2,1,0:T(2,128)(2,1)} reshape(bf16[192,2048]{1,0:T(8,128)(2,1)} %get-tuple-element.5) | data formatting | bytes 1572864 | tf_op jit(solution)/shard_map/squeeze | solution.py:58
  49.9 3.0 %reshape.79 = f32[4,24,2,2048]{3,2,1,0:T(2,128)} reshape(f32[192,2048]{1,0:T(8,128)} %get-tuple-element.6) | data formatting | bytes 3145728 | tf_op jit(solution)/shard_map/convert_element_type | solution.py:59
  52.9 3.3 %add_convert_fusion = bf16[4,24,2,2048]{3,2,1,0:T(2,128)(2,1)} fusion(f32[4,24,2,2048]{3,2,1,0:T(2,128)} %reshape.79, bf16[4,24,2,2048]{3,2,1,0:T(2,128)(2,1)} %collective-permute-done.1), kind=kLoop, calls=%fused_computation.7 | loop fusion | flops 1179648 | bytes 3145728 | tf_op jit(solution)/shard_map/convert_element_type | solution.py:59
  56.3 4.5 %all-to-all-start.1 = ((bf16[4,24,2,2048]{3,2,1,0:T(2,128)(2,1)}), bf16[4,24,2,2048]{3,2,1,0:T(2,128)(2,1)}, u32[]{:S(2)}, u32[]{:S(2)}) async-start(bf16[4,24,2,2048]{3,2,1,0:T(2,128)(2,1)} %add_convert_fusion), calls=%async_computation.1 | async-start | bytes 1572864 | tf_op jit(solution)/shard_map/all_to_all | solution.py:60
  61.2 20.4 %all-to-all-done.1 = bf16[4,24,2,2048]{3,2,1,0:T(2,128)(2,1)} async-done(((bf16[4,24,2,2048]{3,2,1,0:T(2,128)(2,1)}), bf16[4,24,2,2048]{3,2,1,0:T(2,128)(2,1)}, u32[]{:S(2)}, u32[]{:S(2)}) %all-to-all-start.1) | async-done | bytes 786464 | tf_op jit(solution)/shard_map/all_to_all | solution.py:60
  81.6 2.3 %copy.24 = bf16[4,24,2,2048]{3,1,0,2:T(8,128)(2,1)} copy(bf16[4,24,2,2048]{3,2,1,0:T(2,128)(2,1)} %all-to-all-done.1) | data formatting | bytes 1572864 | tf_op jit(solution)/shard_map/all_to_all | solution.py:60
  83.8 3.6 %gather_fusion = bf16[128,2048]{1,0:T(8,128)(2,1)} fusion(bf16[2,96,2048]{2,1,0:T(8,128)(2,1)} %bitcast.39, s32[128]{0:T(128)S(1)} %reshape.81), kind=kCustom, calls=%fused_computation | custom fusion | bytes 1049600 | tf_op jit(solution)/shard_map/gather | solution.py:63
  87.5 2.7 %reshape.80 = f32[2,32,2,2048]{3,2,1,0:T(2,128)} reshape(bf16[128,2048]{1,0:T(8,128)(2,1)} %gather_fusion) | data formatting | bytes 1572864 | tf_op jit(solution)/shard_map/convert_element_type | solution.py:65
  90.2 2.8 %multiply_reduce_fusion = f32[2,32,2048]{2,1,0:T(8,128)S(1)} fusion(f32[2,32,2,2048]{3,2,1,0:T(2,128)} %reshape.80, f32[2,32,2]{2,1,0:T(8,128)S(1)} %copy.20), kind=kLoop, calls=%fused_computation.8 | loop fusion | flops 393216 | bytes 1573376 | tf_op jit(solution)/shard_map/reduce_sum | solution.py:64
  93.1 1.5 %collective-permute-start.2 = (bf16[2,32,2048]{2,1,0:T(8,128)(2,1)S(1)}, bf16[2,32,2048]{2,1,0:T(8,128)(2,1)S(1)}, u32[]{:S(2)}, u32[]{:S(2)}) collective-permute-start(bf16[2,32,2048]{2,1,0:T(8,128)(2,1)S(1)} %fusion.7), channel_id=1, source_target_pairs={{0,8},{8,16},{16,24},{24,0},{1,9},{9,17},{17,25},{25,1},{2,10},{10... | collective-permute-start | bytes 786440 | tf_op jit(solution)/shard_map/ppermute | solution.py:13
  94.6 7.1 %collective-permute-done.2 = bf16[2,32,2048]{2,1,0:T(8,128)(2,1)S(1)} collective-permute-done((bf16[2,32,2048]{2,1,0:T(8,128)(2,1)S(1)}, bf16[2,32,2048]{2,1,0:T(8,128)(2,1)S(1)}, u32[]{:S(2)}, u32[]{:S(2)}) %collective-permute-start.2) | collective-permute-done | bytes 262176 | tf_op jit(solution)/shard_map/ppermute | solution.py:13
  101.8 0.7 copy.27
  (28 shorter events, 1.4 us)
Async XLA Ops:
  0.0 41.3 %copy-start = (bf16[1,1,2048,768]{3,2,1,0:T(8,128)(2,1)S(1)}, bf16[1,1,2048,768]{3,2,1,0:T(8,128)(2,1)}, u32[]{:S(2)}) copy-start(bf16[1,1,2048,768]{3,2,1,0:T(8,128)(2,1)} %param.10) | copy-start | bytes 9437188
  32.0 2.3 %collective-permute-start = (bf16[4,24,2,2048]{3,2,1,0:T(2,128)(2,1)S(1)}, bf16[4,24,2,2048]{3,2,1,0:T(2,128)(2,1)S(1)}, u32[]{:S(2)}, u32[]{:S(2)}) collective-permute-start(bf16[4,24,2,2048]{3,2,1,0:T(2,128)(2,1)S(1)} %all_to_all.10), channel_id=1, source_target_pairs={{0,1},{1,0},{2,3},{3,2},{4,5},{5,4},{6,7},{7,6},{8,9},{9,8},{10,11... | collective-permute-start | bytes 2359304 | tf_op jit(solution)/shard_map/ppermute | solution.py:17
  41.3 2.9 %copy-start.4 = (bf16[1,1,384,2048]{3,2,1,0:T(8,128)(2,1)S(1)}, bf16[1,1,384,2048]{3,2,1,0:T(8,128)(2,1)}, u32[]{:S(2)}) copy-start(bf16[1,1,384,2048]{3,2,1,0:T(8,128)(2,1)} %param.11) | copy-start | bytes 4718596
  49.7 3.2 %collective-permute-start.1 = (bf16[4,24,2,2048]{3,2,1,0:T(2,128)(2,1)}, bf16[4,24,2,2048]{3,2,1,0:T(2,128)(2,1)}, u32[]{:S(2)}, u32[]{:S(2)}) collective-permute-start(bf16[4,24,2,2048]{3,2,1,0:T(2,128)(2,1)} %squeeze.13), channel_id=1, source_target_pairs={{0,1},{1,0},{2,3},{3,2},{4,5},{5,4},{6,7},{7,6},{8,9},{9,8},{10,11... | collective-permute-start | bytes 2359304 | tf_op jit(solution)/shard_map/ppermute | solution.py:17
  56.3 4.5 %copy-start.2 = (s32[1,2,32,2]{2,3,1,0:T(2,128)S(1)}, s32[1,2,32,2]{2,3,1,0:T(2,128)}, u32[]{:S(2)}) copy-start(s32[1,2,32,2]{2,3,1,0:T(2,128)} %param.7) | copy-start | bytes 1540
  56.3 4.8 %copy-start.3 = (f32[1,2,32,2]{2,3,1,0:T(2,128)S(1)}, f32[1,2,32,2]{2,3,1,0:T(2,128)}, u32[]{:S(2)}) copy-start(f32[1,2,32,2]{2,3,1,0:T(2,128)} %param.8) | copy-start | bytes 1540
  56.3 25.3 %all-to-all-start.1 = ((bf16[4,24,2,2048]{3,2,1,0:T(2,128)(2,1)}), bf16[4,24,2,2048]{3,2,1,0:T(2,128)(2,1)}, u32[]{:S(2)}, u32[]{:S(2)}) async-start(bf16[4,24,2,2048]{3,2,1,0:T(2,128)(2,1)} %add_convert_fusion), calls=%async_computation.1 | async-start | bytes 1572864 | tf_op jit(solution)/shard_map/all_to_all | solution.py:60
  87.5 5.5 %copy-start.1 = (bf16[1,2,32,2048]{3,2,1,0:T(8,128)(2,1)S(1)}, bf16[1,2,32,2048]{3,2,1,0:T(8,128)(2,1)}, u32[]{:S(2)}) copy-start(bf16[1,2,32,2048]{3,2,1,0:T(8,128)(2,1)} %param.6) | copy-start | bytes 786436
  93.1 8.7 %collective-permute-start.2 = (bf16[2,32,2048]{2,1,0:T(8,128)(2,1)S(1)}, bf16[2,32,2048]{2,1,0:T(8,128)(2,1)S(1)}, u32[]{:S(2)}, u32[]{:S(2)}) collective-permute-start(bf16[2,32,2048]{2,1,0:T(8,128)(2,1)S(1)} %fusion.7), channel_id=1, source_target_pairs={{0,8},{8,16},{16,24},{24,0},{1,9},{9,17},{17,25},{25,1},{2,10},{10... | collective-permute-start | bytes 786440 | tf_op jit(solution)/shard_map/ppermute | solution.py:13

commit v4 on v3

--- a/solution.py
+++ b/solution.py
@@ -45,25 +45,31 @@
     experts = lax.axis_size("z")
     topk = routes.shape[3]
     capacity = 2 * ((3 * tok_count * topk + 4 * experts - 1) // (4 * experts))
-    normed = normalize(inputs, norm_gain[0])
-    codes = jax.vmap(lambda block: slot_codes(block, experts, capacity))(routes[0])
-    lanes = jnp.arange(experts * capacity, dtype=jnp.int32)
-    onehot = jnp.any(codes[..., None] == lanes, axis=2).astype(jnp.bfloat16)
-    buffer = jnp.einsum("mtq,mtd->qmd", onehot, normed, preferred_element_type=jnp.float32)
-    buffer = buffer.astype(jnp.bfloat16).reshape(experts, capacity, micro, width)
+    block = micro * capacity
+    normed = normalize(inputs, norm_gain[0]).reshape(-1, width)
+    codes = jax.vmap(lambda one: slot_codes(one, experts, capacity))(routes[0])
+    chosen = codes // capacity
+    place = chosen * block + jnp.arange(micro, dtype=jnp.int32)[:, None, None] * capacity
+    place = (place + codes % capacity).reshape(micro * tok_count, topk)
+    lanes = jnp.arange(experts * block, dtype=jnp.int32)
+    hits = place[..., None] == lanes
+    onehot = jnp.any(hits, axis=1).astype(jnp.bfloat16)
+    buffer = jnp.einsum("tq,td->qd", onehot, normed, preferred_element_type=jnp.float32)
+    buffer = buffer.astype(jnp.bfloat16).reshape(experts, block, width)
     incoming = lax.all_to_all(buffer, "z", split_axis=0, concat_axis=0, tiled=True)
-    rows = jnp.stack([incoming, swap_cores(incoming)]).reshape(-1, width)
-    parts = expert_half(rows, gate_up[0, 0], down[0, 0])
-    parts = parts.reshape((2,) + incoming.shape)
+    rows = jnp.concatenate([incoming, swap_cores(incoming)]).reshape(-1, width)
+    parts = expert_half(rows, gate_up[0, 0], down[0, 0]).reshape((2,) + incoming.shape)
     other_half = swap_cores(parts[1])
     results = (parts[0].astype(jnp.float32) + other_half.astype(jnp.float32)).astype(jnp.bfloat16)
     returned = lax.all_to_all(results, "z", split_axis=0, concat_axis=0, tiled=True)
-    table = jnp.swapaxes(returned.reshape(experts * capacity, micro, width), 0, 1)
-    flat_codes = codes.reshape(micro, tok_count * topk)
-    picked = table[jnp.arange(micro)[:, None], flat_codes].reshape(micro, tok_count, topk, width)
-    mixed = inputs.astype(jnp.float32) + jnp.sum(
-        combine_weights[0][..., None] * picked.astype(jnp.float32), axis=2
-    )
+    table = returned.reshape(-1, width)
+    weights = combine_weights[0].reshape(micro * tok_count, topk)
+    mixing = jnp.sum(jnp.where(hits, weights[..., None], 0.0), axis=1)
+    high = mixing.astype(jnp.bfloat16)
+    low = (mixing - high.astype(jnp.float32)).astype(jnp.bfloat16)
+    combined = jnp.dot(high, table, preferred_element_type=jnp.float32)
+    combined = combined + jnp.dot(low, table, preferred_element_type=jnp.float32)
+    mixed = inputs.astype(jnp.float32) + combined.reshape(micro, tok_count, width)
     moved = from_behind(mixed.astype(jnp.bfloat16), "section", 1)
     return moved[None]
 

time: 103 us -> 77.5 us (0.75)
  local copies, waits for them, and re-layouts: 21.3 us -> 2.43 us
  other arithmetic: 13.5 us -> 4.87 us
  waiting for transfers between devices: 29.8 us -> 31.9 us
    convert_element_type x2 -> x0, local copies, waits for them, and re-layouts: 5.75 us -> none  [the longest x1 3.02 us: local(): parts[0].astype(jnp.float32) + other_half.astype(jnp.float32)]
    reshape x2 -> x0, local copies, waits for them, and re-layouts: 4.46 us -> none  [the longest x1 3.65 us: local(): rows = jnp.stack([incoming, swap_cores(incoming)]).reshape(-1, width)]
    gather x1 -> x0, local copies, waits for them, and re-layouts: 3.65 us -> none  [local(): table[jnp.arange(micro)[:, None], flat_codes]]
    another operation x1 -> x0, other arithmetic: 3.44 us -> none  [local(): rows = jnp.stack([incoming, swap_cores(incoming)]).reshape(-1, width)]
    squeeze x1 -> x0, local copies, waits for them, and re-layouts: 2.84 us -> none  [local(): other_half = swap_cores(parts[1])]
    reduce_sum x1, other arithmetic: 2.79 us -> 0.1 us  [local(): mixing = jnp.sum(jnp.where(hits, weights[..., None], 0.0), axis=1)]
    all_to_all x1 -> x0, local copies, waits for them, and re-layouts: 2.29 us -> none  [local(): lax.all_to_all(results, 'z', split_axis=0, concat_axis=0, tiled=True)]
    ppermute x2, waiting for transfers between devices: 2.29 us -> 4.44 us  [swap_cores(): return lax.ppermute(value, 'core', [(0, 1), (1, 0)])]
  transfers between devices with their start and end apart: 4 -> 4, of which waited for: 3 -> 4; matrix products, arithmetic and copies ran while one was open for 3% -> 0% of each run, Pallas kernels for 0% -> 0%
where the time goes in v4:
time: 77.5 us; the launch traced here: 77.2 us
  waiting for transfers between devices  31.9 us (41%)
  blocking collectives  26.3 us (34%)
  starting transfers between devices  5.94 us (8%)
  matrix products  5.64 us (7%)
  other arithmetic  4.87 us (6%)
  local copies, waits for them, and re-layouts  2.43 us (3%)
    all_to_all x1, blocking collectives, local(): lax.all_to_all(buffer, 'z', split_axis=0, concat_axis=0, tiled=True)  26.3 us
    all_to_all x1, waiting for transfers between devices, local(): lax.all_to_all(results, 'z', split_axis=0, concat_axis=0, tiled=True)  20.5 us
    ppermute x1, waiting for transfers between devices, from_behind(): return lax.ppermute(value, axis, pairs)  6.89 us
    ppermute x2, waiting for transfers between devices, swap_cores(): return lax.ppermute(value, 'core', [(0, 1), (1, 0)])  4.44 us
    all_to_all x1, starting transfers between devices, local(): lax.all_to_all(results, 'z', split_axis=0, concat_axis=0, tiled=True)  4.19 us
    unnamed x11, local copies, waits for them, and re-layouts  1.64 us
    ppermute x1, starting transfers between devices, from_behind(): return lax.ppermute(value, axis, pairs)  1.55 us
  transfers between devices with their start and end apart: 4, of which 4 were waited for; matrix products, arithmetic and copies ran while one was open for 0% of the time, Pallas kernels for 0%

profile of v4, /device:TPU:0, one launch (start us, length us, event | category | flops | bytes accessed | tf_op | source)
XLA Modules:
  0.0 77.2 jit_solution(14809020482652940622)
XLA Ops:
  0.0 0.9 %copy.20 = s32[1,2,32,2]{3,2,1,0:T(8,128)S(1)} copy(s32[1,2,32,2]{2,3,1,0:T(2,128)} %param.7) | data formatting | bytes 1024 | tf_op args[1]
  0.9 0.7 broadcast_multiply_fusion
  2.0 0.2 select_reduce_fusion.1
  2.1 0.1 reduce_sum.30
  2.7 1.1 %fusion.7 = f32[2,32]{1,0:T(2,128)S(1)} fusion(bf16[1,2,32,2048]{3,2,1,0:T(8,128)(2,1)} %param.6), kind=kLoop, calls=%fused_computation.16 | loop fusion | flops 393152 | bytes 262400 | tf_op jit(solution)/shard_map/reduce_sum | solution.py:30
  3.9 1.1 %fusion.6 = bf16[64,2048]{1,0:T(8,128)(2,1)S(1)} fusion(bf16[1,2,32,2048]{3,2,1,0:T(8,128)(2,1)} %param.6, f32[2048]{0:T(1024)} %bitcast.45, f32[64]{0:T(128)S(1)} %rsqrt.12), kind=kLoop, calls=%fused_computation.13 | loop fusion | flops 524288 | bytes 532736 | tf_op jit(solution)/shard_map/convert_element_type | solution.py:31
  5.0 0.4 convolution_convert_fusion.1
  5.4 26.3 %all_to_all.10 = bf16[4,48,2048]{2,1,0:T(8,128)(2,1)S(1)} all-to-all(bf16[4,48,2048]{2,1,0:T(8,128)(2,1)S(1)} %bitcast.39), channel_id=1, replica_groups=mesh['section'=4,'z'=4,'core'=2] {'z'}, dimensions={0} | all-to-all | bytes 1572864 | tf_op jit(solution)/shard_map/all_to_all | solution.py:59
  31.6 2.3 %collective-permute-done = bf16[4,48,2048]{2,1,0:T(8,128)(2,1)S(1)} collective-permute-done((bf16[4,48,2048]{2,1,0:T(8,128)(2,1)S(1)}, bf16[4,48,2048]{2,1,0:T(8,128)(2,1)S(1)}, u32[]{:S(2)}, u32[]{:S(2)}) %collective-permute-start) | collective-permute-done | bytes 786464 | tf_op jit(solution)/shard_map/ppermute | solution.py:17
  33.9 0.1 pad_maximum_fusion
  34.1 1.4 %fusion = f32[384,768]{1,0:T(8,128)S(1)} fusion(bf16[384,2048]{1,0:T(8,128)(2,1)S(1)} %bitcast.42, bf16[1,1,2048,768]{3,2,1,0:T(8,128)(2,1)S(1)} %copy-done), kind=kOutput, calls=%fused_computation | convolution fusion | flops 1207959552 | bytes 5898240 | tf_op jit(solution)/shard_map/dot_general | solution.py:36
  35.5 1.0 %convolution_convert_fusion = bf16[384,2048]{1,0:T(8,128)(2,1)S(1)} fusion(bf16[1,1,384,2048]{3,2,1,0:T(8,128)(2,1)S(1)} %copy-done.3, f32[384,768]{1,0:T(8,128)S(1)} %fusion), kind=kOutput, calls=%fused_computation.2 | convolution fusion | flops 605650944 | bytes 4325376 | tf_op jit(solution)/shard_map/dot_general | solution.py:38
  36.5 0.1 fusion.18
  36.6 0.2 collective-permute-start.1
  36.8 2.2 %collective-permute-done.1 = bf16[4,48,2048]{2,1,0:T(8,128)(2,1)S(1)} collective-permute-done((bf16[4,48,2048]{2,1,0:T(8,128)(2,1)S(1)}, bf16[4,48,2048]{2,1,0:T(8,128)(2,1)S(1)}, u32[]{:S(2)}, u32[]{:S(2)}) %collective-permute-start.1) | collective-permute-done | bytes 786464 | tf_op jit(solution)/shard_map/ppermute | solution.py:17
  39.0 1.2 %fusion.2 = bf16[4,48,2048]{2,1,0:T(8,128)(2,1)} fusion(bf16[4,48,2048]{2,1,0:T(8,128)(2,1)S(1)} %bitcast.40, bf16[4,48,2048]{2,1,0:T(8,128)(2,1)S(1)} %collective-permute-done.1), kind=kLoop, calls=%fused_computation.7 | loop fusion | flops 1572864 | bytes 2359296 | tf_op jit(solution)/shard_map/convert_element_type | solution.py:63
  40.2 4.2 %all-to-all-start.1 = ((bf16[4,48,2048]{2,1,0:T(8,128)(2,1)}), bf16[4,48,2048]{2,1,0:T(8,128)(2,1)}, u32[]{:S(2)}, u32[]{:S(2)}) async-start(bf16[4,48,2048]{2,1,0:T(8,128)(2,1)} %fusion.2), calls=%async_computation.1 | async-start | bytes 1572864 | tf_op jit(solution)/shard_map/all_to_all | solution.py:64
  44.5 0.1 select_reduce_fusion
  44.6 20.5 %all-to-all-done.1 = bf16[4,48,2048]{2,1,0:T(8,128)(2,1)} async-done(((bf16[4,48,2048]{2,1,0:T(8,128)(2,1)}), bf16[4,48,2048]{2,1,0:T(8,128)(2,1)}, u32[]{:S(2)}, u32[]{:S(2)}) %all-to-all-start.1) | async-done | bytes 786464 | tf_op jit(solution)/shard_map/all_to_all | solution.py:64
  65.1 1.4 %fusion.14 = f32[64,2048]{1,0:T(8,128)S(1)} fusion(bf16[192,2048]{1,0:T(8,128)(2,1)} %bitcast.9, f32[64,192]{1,0:T(8,128)S(1)} %select_reduce_fusion), kind=kOutput, calls=%fused_computation.27 | convolution fusion | flops 50343936 | bytes 1359872 | tf_op jit(solution)/shard_map/dot_general | solution.py:70
  66.6 1.4 %convolution_add_fusion = f32[64,2048]{1,0:T(8,128)S(1)} fusion(f32[64,2048]{1,0:T(8,128)S(1)} %fusion.14, bf16[192,2048]{1,0:T(8,128)(2,1)} %bitcast.9, f32[64,192]{1,0:T(8,128)S(1)} %select_reduce_fusion), kind=kOutput, calls=%fused_computation.4 | convolution fusion | flops 50511872 | bytes 1884160 | tf_op jit(solution)/shard_map/dot_general | solution.py:71
  68.0 1.6 %collective-permute-start.2 = (bf16[2,32,2048]{2,1,0:T(8,128)(2,1)S(1)}, bf16[2,32,2048]{2,1,0:T(8,128)(2,1)S(1)}, u32[]{:S(2)}, u32[]{:S(2)}) collective-permute-start(bf16[2,32,2048]{2,1,0:T(8,128)(2,1)S(1)} %fusion.8), channel_id=1, source_target_pairs={{0,8},{8,16},{16,24},{24,0},{1,9},{9,17},{17,25},{25,1},{2,10},{10... | collective-permute-start | bytes 786440 | tf_op jit(solution)/shard_map/ppermute | solution.py:13
  69.6 6.9 %collective-permute-done.2 = bf16[2,32,2048]{2,1,0:T(8,128)(2,1)S(1)} collective-permute-done((bf16[2,32,2048]{2,1,0:T(8,128)(2,1)S(1)}, bf16[2,32,2048]{2,1,0:T(8,128)(2,1)S(1)}, u32[]{:S(2)}, u32[]{:S(2)}) %collective-permute-start.2) | collective-permute-done | bytes 262176 | tf_op jit(solution)/shard_map/ppermute | solution.py:13
  76.5 0.7 copy.24
  (25 shorter events, 1.0 us)
Async XLA Ops:
  0.0 34.1 %copy-start = (bf16[1,1,2048,768]{3,2,1,0:T(8,128)(2,1)S(1)}, bf16[1,1,2048,768]{3,2,1,0:T(8,128)(2,1)}, u32[]{:S(2)}) copy-start(bf16[1,1,2048,768]{3,2,1,0:T(8,128)(2,1)} %param.10) | copy-start | bytes 9437188
  31.6 2.3 %collective-permute-start = (bf16[4,48,2048]{2,1,0:T(8,128)(2,1)S(1)}, bf16[4,48,2048]{2,1,0:T(8,128)(2,1)S(1)}, u32[]{:S(2)}, u32[]{:S(2)}) collective-permute-start(bf16[4,48,2048]{2,1,0:T(8,128)(2,1)S(1)} %all_to_all.10), channel_id=1, source_target_pairs={{0,1},{1,0},{2,3},{3,2},{4,5},{5,4},{6,7},{7,6},{8,9},{9,8},{10,11... | collective-permute-start | bytes 2359304 | tf_op jit(solution)/shard_map/ppermute | solution.py:17
  34.1 1.4 %copy-start.3 = (bf16[1,1,384,2048]{3,2,1,0:T(8,128)(2,1)S(1)}, bf16[1,1,384,2048]{3,2,1,0:T(8,128)(2,1)}, u32[]{:S(2)}) copy-start(bf16[1,1,384,2048]{3,2,1,0:T(8,128)(2,1)} %param.11) | copy-start | bytes 4718596
  36.6 2.4 %collective-permute-start.1 = (bf16[4,48,2048]{2,1,0:T(8,128)(2,1)S(1)}, bf16[4,48,2048]{2,1,0:T(8,128)(2,1)S(1)}, u32[]{:S(2)}, u32[]{:S(2)}) collective-permute-start(bf16[4,48,2048]{2,1,0:T(8,128)(2,1)S(1)} %bitcast.43), channel_id=1, source_target_pairs={{0,1},{1,0},{2,3},{3,2},{4,5},{5,4},{6,7},{7,6},{8,9},{9,8},{10,11... | collective-permute-start | bytes 2359304 | tf_op jit(solution)/shard_map/ppermute | solution.py:17
  39.0 5.4 %copy-start.2 = (f32[1,2,32,2]{2,3,1,0:T(2,128)S(1)}, f32[1,2,32,2]{2,3,1,0:T(2,128)}, u32[]{:S(2)}) copy-start(f32[1,2,32,2]{2,3,1,0:T(2,128)} %param.8) | copy-start | bytes 1540
  40.2 24.9 %all-to-all-start.1 = ((bf16[4,48,2048]{2,1,0:T(8,128)(2,1)}), bf16[4,48,2048]{2,1,0:T(8,128)(2,1)}, u32[]{:S(2)}, u32[]{:S(2)}) async-start(bf16[4,48,2048]{2,1,0:T(8,128)(2,1)} %fusion.2), calls=%async_computation.1 | async-start | bytes 1572864 | tf_op jit(solution)/shard_map/all_to_all | solution.py:64
  65.1 2.8 %copy-start.1 = (bf16[1,2,32,2048]{3,2,1,0:T(8,128)(2,1)S(1)}, bf16[1,2,32,2048]{3,2,1,0:T(8,128)(2,1)}, u32[]{:S(2)}) copy-start(bf16[1,2,32,2048]{3,2,1,0:T(8,128)(2,1)} %param.6) | copy-start | bytes 786436
  68.0 8.4 %collective-permute-start.2 = (bf16[2,32,2048]{2,1,0:T(8,128)(2,1)S(1)}, bf16[2,32,2048]{2,1,0:T(8,128)(2,1)S(1)}, u32[]{:S(2)}, u32[]{:S(2)}) collective-permute-start(bf16[2,32,2048]{2,1,0:T(8,128)(2,1)S(1)} %fusion.8), channel_id=1, source_target_pairs={{0,8},{8,16},{16,24},{24,0},{1,9},{9,17},{17,25},{25,1},{2,10},{10... | collective-permute-start | bytes 786440 | tf_op jit(solution)/shard_map/ppermute | solution.py:13

commit v5 on v4

--- a/solution.py
+++ b/solution.py
@@ -57,18 +57,22 @@
     buffer = jnp.einsum("tq,td->qd", onehot, normed, preferred_element_type=jnp.float32)
     buffer = buffer.astype(jnp.bfloat16).reshape(experts, block, width)
     incoming = lax.all_to_all(buffer, "z", split_axis=0, concat_axis=0, tiled=True)
-    rows = jnp.concatenate([incoming, swap_cores(incoming)]).reshape(-1, width)
-    parts = expert_half(rows, gate_up[0, 0], down[0, 0]).reshape((2,) + incoming.shape)
-    other_half = swap_cores(parts[1])
-    results = (parts[0].astype(jnp.float32) + other_half.astype(jnp.float32)).astype(jnp.bfloat16)
+    partner_rows = swap_cores(incoming)
+    own = expert_half(incoming.reshape(-1, width), gate_up[0, 0], down[0, 0])
+    lent = expert_half(partner_rows.reshape(-1, width), gate_up[0, 0], down[0, 0])
+    other_half = swap_cores(lent.reshape(incoming.shape))
+    results = (own.reshape(incoming.shape).astype(jnp.float32) + other_half.astype(jnp.float32))
+    results = results.astype(jnp.bfloat16)
     returned = lax.all_to_all(results, "z", split_axis=0, concat_axis=0, tiled=True)
     table = returned.reshape(-1, width)
     weights = combine_weights[0].reshape(micro * tok_count, topk)
     mixing = jnp.sum(jnp.where(hits, weights[..., None], 0.0), axis=1)
-    high = mixing.astype(jnp.bfloat16)
-    low = (mixing - high.astype(jnp.float32)).astype(jnp.bfloat16)
-    combined = jnp.dot(high, table, preferred_element_type=jnp.float32)
-    combined = combined + jnp.dot(low, table, preferred_element_type=jnp.float32)
+    combined = jnp.dot(
+        mixing,
+        table.astype(jnp.float32),
+        precision=lax.Precision.HIGHEST,
+        preferred_element_type=jnp.float32,
+    )
     mixed = inputs.astype(jnp.float32) + combined.reshape(micro, tok_count, width)
     moved = from_behind(mixed.astype(jnp.bfloat16), "section", 1)
     return moved[None]

time: 77.5 us -> 75.6 us (0.975)
  waiting for transfers between devices: 31.9 us -> 30.5 us
  matrix products: 5.64 us -> 4.81 us
    ppermute x2, waiting for transfers between devices: 4.44 us -> 3.05 us  [swap_cores(): return lax.ppermute(value, 'core', [(0, 1), (1, 0)])]
    dot_general x2 -> x1, matrix products: 2.83 us -> 1.67 us  [local(): jnp.dot(mixing, table.astype(jnp.float32), precision=lax.Precision.HIGHES...]
    dot_general x1 -> x2, matrix products: 1.42 us -> 1.55 us  [expert_half(): joined = jnp.dot(token_rows, weights_gu, preferred_element_type=jnp.float32)]
  transfers between devices with their start and end apart: 4 -> 4, of which waited for: 4 -> 4; matrix products, arithmetic and copies ran while one was open for 0% -> 2% of each run, Pallas kernels for 0% -> 0%
where the time goes in v5:
time: 75.6 us; the launch traced here: 75.2 us
  waiting for transfers between devices  30.5 us (40%)
  blocking collectives  26.3 us (35%)
  starting transfers between devices  5.93 us (8%)
  matrix products  4.81 us (6%)
  other arithmetic  4.68 us (6%)
  local copies, waits for them, and re-layouts  2.94 us (4%)
    all_to_all x1, blocking collectives, local(): lax.all_to_all(buffer, 'z', split_axis=0, concat_axis=0, tiled=True)  26.3 us
    all_to_all x1, waiting for transfers between devices, local(): lax.all_to_all(results, 'z', split_axis=0, concat_axis=0, tiled=True)  20.5 us
    ppermute x1, waiting for transfers between devices, from_behind(): return lax.ppermute(value, axis, pairs)  6.9 us
    all_to_all x1, starting transfers between devices, local(): lax.all_to_all(results, 'z', split_axis=0, concat_axis=0, tiled=True)  4.19 us
    ppermute x2, waiting for transfers between devices, swap_cores(): return lax.ppermute(value, 'core', [(0, 1), (1, 0)])  3.05 us
    unnamed x11, local copies, waits for them, and re-layouts  2.26 us
    dot_general x1, matrix products, local(): jnp.dot(mixing, table.astype(jnp.float32), precision=lax.Precision.HIGHES...  1.67 us
    dot_general x2, matrix products, expert_half(): joined = jnp.dot(token_rows, weights_gu, preferred_element_type=jnp.float32)  1.55 us
  transfers between devices with their start and end apart: 4, of which 4 were waited for; matrix products, arithmetic and copies ran while one was open for 2% of the time, Pallas kernels for 0%

profile of v5, /device:TPU:0, one launch (start us, length us, event | category | flops | bytes accessed | tf_op | source)
XLA Modules:
  0.0 75.2 jit_solution(13120394288372498570)
XLA Ops:
  0.0 0.9 %copy.20 = s32[1,2,32,2]{3,2,1,0:T(8,128)S(1)} copy(s32[1,2,32,2]{2,3,1,0:T(2,128)} %param.7) | data formatting | bytes 1024 | tf_op args[1]
  0.9 0.7 broadcast_multiply_fusion
  2.0 0.2 select_reduce_fusion.1
  2.1 0.1 reduce_sum.30
  2.7 1.1 %fusion.10 = f32[2,32]{1,0:T(2,128)S(1)} fusion(bf16[1,2,32,2048]{3,2,1,0:T(8,128)(2,1)} %param.6), kind=kLoop, calls=%fused_computation.17 | loop fusion | flops 393152 | bytes 262400 | tf_op jit(solution)/shard_map/reduce_sum | solution.py:30
  3.9 1.1 %fusion.9 = bf16[64,2048]{1,0:T(8,128)(2,1)S(1)} fusion(bf16[1,2,32,2048]{3,2,1,0:T(8,128)(2,1)} %param.6, f32[2048]{0:T(1024)} %bitcast.51, f32[64]{0:T(128)S(1)} %rsqrt.12), kind=kLoop, calls=%fused_computation.15 | loop fusion | flops 524288 | bytes 532736 | tf_op jit(solution)/shard_map/convert_element_type | solution.py:31
  5.0 0.4 convolution_convert_fusion
  5.4 26.3 %all_to_all.10 = bf16[4,48,2048]{2,1,0:T(8,128)(2,1)S(1)} all-to-all(bf16[4,48,2048]{2,1,0:T(8,128)(2,1)S(1)} %bitcast.45), channel_id=1, replica_groups=mesh['section'=4,'z'=4,'core'=2] {'z'}, dimensions={0} | all-to-all | bytes 1572864 | tf_op jit(solution)/shard_map/all_to_all | solution.py:59
  31.6 2.3 %collective-permute-done = bf16[4,48,2048]{2,1,0:T(8,128)(2,1)S(1)} collective-permute-done((bf16[4,48,2048]{2,1,0:T(8,128)(2,1)S(1)}, bf16[4,48,2048]{2,1,0:T(8,128)(2,1)S(1)}, u32[]{:S(2)}, u32[]{:S(2)}) %collective-permute-start) | collective-permute-done | bytes 786464 | tf_op jit(solution)/shard_map/ppermute | solution.py:17
  33.9 0.8 %fusion = f32[192,768]{1,0:T(8,128)S(1)} fusion(bf16[192,2048]{1,0:T(8,128)(2,1)S(1)} %bitcast.48, bf16[1,1,2048,768]{3,2,1,0:T(8,128)(2,1)S(1)} %copy-done), kind=kOutput, calls=%fused_computation | convolution fusion | flops 603979776 | bytes 4521984 | tf_op jit(solution)/shard_map/dot_general | solution.py:36
  34.7 0.6 copy-done.3
  35.3 0.6 convolution_convert_fusion.1
  35.9 0.2 collective-permute-start.1
  36.1 0.8 %fusion.2 = f32[192,768]{1,0:T(8,128)S(1)} fusion(bf16[192,2048]{1,0:T(8,128)(2,1)S(1)} %bitcast.46, bf16[1,1,2048,768]{3,2,1,0:T(8,128)(2,1)S(1)} %copy-done), kind=kOutput, calls=%fused_computation.2 | convolution fusion | flops 603979776 | bytes 4521984 | tf_op jit(solution)/shard_map/dot_general | solution.py:36
  36.9 0.6 convolution_convert_fusion.2
  37.5 0.8 %collective-permute-done.1 = bf16[4,48,2048]{2,1,0:T(8,128)(2,1)S(1)} collective-permute-done((bf16[4,48,2048]{2,1,0:T(8,128)(2,1)S(1)}, bf16[4,48,2048]{2,1,0:T(8,128)(2,1)S(1)}, u32[]{:S(2)}, u32[]{:S(2)}) %collective-permute-start.1) | collective-permute-done | bytes 786464 | tf_op jit(solution)/shard_map/ppermute | solution.py:17
  38.3 1.2 %fusion.5 = bf16[4,48,2048]{2,1,0:T(8,128)(2,1)} fusion(bf16[4,48,2048]{2,1,0:T(8,128)(2,1)S(1)} %bitcast.47, bf16[4,48,2048]{2,1,0:T(8,128)(2,1)S(1)} %collective-permute-done.1), kind=kLoop, calls=%fused_computation.10 | loop fusion | flops 1572864 | bytes 2359296 | tf_op jit(solution)/shard_map/convert_element_type | solution.py:65
  39.5 4.2 %all-to-all-start.1 = ((bf16[4,48,2048]{2,1,0:T(8,128)(2,1)}), bf16[4,48,2048]{2,1,0:T(8,128)(2,1)}, u32[]{:S(2)}, u32[]{:S(2)}) async-start(bf16[4,48,2048]{2,1,0:T(8,128)(2,1)} %fusion.5), calls=%async_computation.1 | async-start | bytes 1572864 | tf_op jit(solution)/shard_map/all_to_all | solution.py:66
  43.8 0.1 select_reduce_fusion
  43.9 20.5 %all-to-all-done.1 = bf16[4,48,2048]{2,1,0:T(8,128)(2,1)} async-done(((bf16[4,48,2048]{2,1,0:T(8,128)(2,1)}), bf16[4,48,2048]{2,1,0:T(8,128)(2,1)}, u32[]{:S(2)}, u32[]{:S(2)}) %all-to-all-start.1) | async-done | bytes 786464 | tf_op jit(solution)/shard_map/all_to_all | solution.py:66
  64.4 1.7 %fusion.4 = bf16[2,32,2048]{2,1,0:T(8,128)(2,1)S(1)} fusion(f32[2,32,192]{2,1,0:T(8,128)S(1)} %bitcast.50, bf16[192,2048,1]{1,0,2:T(8,128)(2,1)} %bitcast.12, bf16[1,2,32,2048]{3,2,1,0:T(8,128)(2,1)S(1)} %copy-done.1), kind=kOutput, calls=%fused_computation.8 | convolution fusion | flops 302383104 | bytes 1359872 | tf_op jit(solution)/shard_map/dot_general | solution.py:70
  66.1 1.5 %collective-permute-start.2 = (bf16[2,32,2048]{2,1,0:T(8,128)(2,1)S(1)}, bf16[2,32,2048]{2,1,0:T(8,128)(2,1)S(1)}, u32[]{:S(2)}, u32[]{:S(2)}) collective-permute-start(bf16[2,32,2048]{2,1,0:T(8,128)(2,1)S(1)} %fusion.4), channel_id=1, source_target_pairs={{0,8},{8,16},{16,24},{24,0},{1,9},{9,17},{17,25},{25,1},{2,10},{10... | collective-permute-start | bytes 786440 | tf_op jit(solution)/shard_map/ppermute | solution.py:13
  67.6 6.9 %collective-permute-done.2 = bf16[2,32,2048]{2,1,0:T(8,128)(2,1)S(1)} collective-permute-done((bf16[2,32,2048]{2,1,0:T(8,128)(2,1)S(1)}, bf16[2,32,2048]{2,1,0:T(8,128)(2,1)S(1)}, u32[]{:S(2)}, u32[]{:S(2)}) %collective-permute-start.2) | collective-permute-done | bytes 262176 | tf_op jit(solution)/shard_map/ppermute | solution.py:13
  74.5 0.7 copy.24
  (23 shorter events, 0.9 us)
Async XLA Ops:
  0.0 33.9 %copy-start = (bf16[1,1,2048,768]{3,2,1,0:T(8,128)(2,1)S(1)}, bf16[1,1,2048,768]{3,2,1,0:T(8,128)(2,1)}, u32[]{:S(2)}) copy-start(bf16[1,1,2048,768]{3,2,1,0:T(8,128)(2,1)} %param.10) | copy-start | bytes 9437188
  31.6 2.3 %collective-permute-start = (bf16[4,48,2048]{2,1,0:T(8,128)(2,1)S(1)}, bf16[4,48,2048]{2,1,0:T(8,128)(2,1)S(1)}, u32[]{:S(2)}, u32[]{:S(2)}) collective-permute-start(bf16[4,48,2048]{2,1,0:T(8,128)(2,1)S(1)} %all_to_all.10), channel_id=1, source_target_pairs={{0,1},{1,0},{2,3},{3,2},{4,5},{5,4},{6,7},{7,6},{8,9},{9,8},{10,11... | collective-permute-start | bytes 2359304 | tf_op jit(solution)/shard_map/ppermute | solution.py:17
  33.9 1.4 %copy-start.3 = (bf16[1,1,384,2048]{3,2,1,0:T(8,128)(2,1)S(1)}, bf16[1,1,384,2048]{3,2,1,0:T(8,128)(2,1)}, u32[]{:S(2)}) copy-start(bf16[1,1,384,2048]{3,2,1,0:T(8,128)(2,1)} %param.11) | copy-start | bytes 4718596
  35.9 2.4 %collective-permute-start.1 = (bf16[4,48,2048]{2,1,0:T(8,128)(2,1)S(1)}, bf16[4,48,2048]{2,1,0:T(8,128)(2,1)S(1)}, u32[]{:S(2)}, u32[]{:S(2)}) collective-permute-start(bf16[4,48,2048]{2,1,0:T(8,128)(2,1)S(1)} %bitcast.52), channel_id=1, source_target_pairs={{0,1},{1,0},{2,3},{3,2},{4,5},{5,4},{6,7},{7,6},{8,9},{9,8},{10,11... | collective-permute-start | bytes 2359304 | tf_op jit(solution)/shard_map/ppermute | solution.py:17
  38.3 5.4 %copy-start.2 = (f32[1,2,32,2]{2,3,1,0:T(2,128)S(1)}, f32[1,2,32,2]{2,3,1,0:T(2,128)}, u32[]{:S(2)}) copy-start(f32[1,2,32,2]{2,3,1,0:T(2,128)} %param.8) | copy-start | bytes 1540
  38.3 26.1 %copy-start.1 = (bf16[1,2,32,2048]{3,2,1,0:T(8,128)(2,1)S(1)}, bf16[1,2,32,2048]{3,2,1,0:T(8,128)(2,1)}, u32[]{:S(2)}) copy-start(bf16[1,2,32,2048]{3,2,1,0:T(8,128)(2,1)} %param.6) | copy-start | bytes 786436
  39.5 24.9 %all-to-all-start.1 = ((bf16[4,48,2048]{2,1,0:T(8,128)(2,1)}), bf16[4,48,2048]{2,1,0:T(8,128)(2,1)}, u32[]{:S(2)}, u32[]{:S(2)}) async-start(bf16[4,48,2048]{2,1,0:T(8,128)(2,1)} %fusion.5), calls=%async_computation.1 | async-start | bytes 1572864 | tf_op jit(solution)/shard_map/all_to_all | solution.py:66
  66.1 8.4 %collective-permute-start.2 = (bf16[2,32,2048]{2,1,0:T(8,128)(2,1)S(1)}, bf16[2,32,2048]{2,1,0:T(8,128)(2,1)S(1)}, u32[]{:S(2)}, u32[]{:S(2)}) collective-permute-start(bf16[2,32,2048]{2,1,0:T(8,128)(2,1)S(1)} %fusion.4), channel_id=1, source_target_pairs={{0,8},{8,16},{16,24},{24,0},{1,9},{9,17},{17,25},{25,1},{2,10},{10... | collective-permute-start | bytes 786440 | tf_op jit(solution)/shard_map/ppermute | solution.py:13

commit v6 on v5

--- a/solution.py
+++ b/solution.py
@@ -63,19 +63,33 @@
     other_half = swap_cores(lent.reshape(incoming.shape))
     results = (own.reshape(incoming.shape).astype(jnp.float32) + other_half.astype(jnp.float32))
     results = results.astype(jnp.bfloat16)
-    returned = lax.all_to_all(results, "z", split_axis=0, concat_axis=0, tiled=True)
-    table = returned.reshape(-1, width)
     weights = combine_weights[0].reshape(micro * tok_count, topk)
     mixing = jnp.sum(jnp.where(hits, weights[..., None], 0.0), axis=1)
-    combined = jnp.dot(
-        mixing,
-        table.astype(jnp.float32),
-        precision=lax.Precision.HIGHEST,
-        preferred_element_type=jnp.float32,
-    )
-    mixed = inputs.astype(jnp.float32) + combined.reshape(micro, tok_count, width)
-    moved = from_behind(mixed.astype(jnp.bfloat16), "section", 1)
-    return moved[None]
+    ahead_inputs = from_behind(inputs, "section", 1)
+    ahead_mixing = from_behind(mixing, "section", 1)
+    sections = lax.axis_size("section")
+    chip = lax.axis_index("z")
+    combined = jnp.zeros((micro * tok_count, width), jnp.float32)
+    for shift in range(1 - experts, experts):
+        target = jnp.clip(chip + shift, 0, experts - 1)
+        piece = lax.dynamic_index_in_dim(results, target, 0, keepdims=False)
+        pairs = [
+            (here * experts + lane, ((here + 1) % sections) * experts + lane + shift)
+            for here in range(sections)
+            for lane in range(experts)
+            if 0 <= lane + shift < experts
+        ]
+        got = lax.ppermute(piece, ("section", "z"), pairs)
+        source = jnp.clip(chip - shift, 0, experts - 1)
+        columns = lax.dynamic_slice_in_dim(ahead_mixing, source * block, block, axis=1)
+        combined = combined + jnp.dot(
+            columns,
+            got.astype(jnp.float32),
+            precision=lax.Precision.HIGHEST,
+            preferred_element_type=jnp.float32,
+        )
+    mixed = ahead_inputs.astype(jnp.float32) + combined.reshape(micro, tok_count, width)
+    return mixed.astype(jnp.bfloat16)[None]
 
 
 def solution(mesh):

time: 75.6 us -> 82.8 us (1.095)
  waiting for transfers between devices: 30.5 us -> 10.7 us
  starting transfers between devices: 5.93 us -> 25.2 us
  matrix products: 4.81 us -> 10.2 us
  local copies, waits for them, and re-layouts: 2.94 us -> 4.24 us
    ppermute x0 -> x7, starting transfers between devices: none -> 22 us  [local(): got = lax.ppermute(piece, ('section', 'z'), pairs)]
    all_to_all x1 -> x0, waiting for transfers between devices: 20.5 us -> none  [local(): lax.all_to_all(results, 'z', split_axis=0, concat_axis=0, tiled=True)]
    ppermute x0 -> x7, waiting for transfers between devices: none -> 8.39 us  [local(): got = lax.ppermute(piece, ('section', 'z'), pairs)]
    ppermute x1 -> x2, waiting for transfers between devices: 6.9 us -> 0.01 us  [from_behind(): return lax.ppermute(value, axis, pairs)]
    all_to_all x1 -> x0, starting transfers between devices: 4.19 us -> none  [local(): lax.all_to_all(results, 'z', split_axis=0, concat_axis=0, tiled=True)]
    dot_general x1 -> x7, matrix products: 1.67 us -> 3.95 us  [local(): jnp.dot(columns, got.astype(jnp.float32), precision=lax.Precision.HIGHEST...]
    broadcast_in_dim x0 -> x1, other arithmetic: none -> 1.7 us  [local(): return mixed.astype(jnp.bfloat16)[None]]
    ppermute x1 -> x2, starting transfers between devices: 1.54 us -> 3.03 us  [from_behind(): return lax.ppermute(value, axis, pairs)]
  transfers between devices with their start and end apart: 4 -> 11, of which waited for: 4 -> 4; matrix products, arithmetic and copies ran while one was open for 2% -> 8% of each run, Pallas kernels for 0% -> 0%
where the time goes in v6:
time: 82.8 us; the launch traced here: 82.4 us
  blocking collectives  26.3 us (32%)
  starting transfers between devices  25.2 us (30%)
  waiting for transfers between devices  10.7 us (13%)
  matrix products  10.2 us (12%)
  other arithmetic  5.5 us (7%)
  local copies, waits for them, and re-layouts  4.24 us (5%)
    all_to_all x1, blocking collectives, local(): lax.all_to_all(buffer, 'z', split_axis=0, concat_axis=0, tiled=True)  26.3 us
    ppermute x7, starting transfers between devices, local(): got = lax.ppermute(piece, ('section', 'z'), pairs)  22 us
    ppermute x7, waiting for transfers between devices, local(): got = lax.ppermute(piece, ('section', 'z'), pairs)  8.39 us
    dot_general x7, matrix products, local(): jnp.dot(columns, got.astype(jnp.float32), precision=lax.Precision.HIGHEST...  3.95 us
    ppermute x2, starting transfers between devices, from_behind(): return lax.ppermute(value, axis, pairs)  3.03 us
    dot_general x2, matrix products, expert_half(): joined = jnp.dot(token_rows, weights_gu, preferred_element_type=jnp.float32)  2.8 us
    unnamed x14, local copies, waits for them, and re-layouts  2.45 us
    ppermute x2, waiting for transfers between devices, swap_cores(): return lax.ppermute(value, 'core', [(0, 1), (1, 0)])  2.29 us
  transfers between devices with their start and end apart: 11, of which 4 were waited for; matrix products, arithmetic and copies ran while one was open for 8% of the time, Pallas kernels for 0%

profile of v6, /device:TPU:0, one launch (start us, length us, event | category | flops | bytes accessed | tf_op | source)
XLA Modules:
  0.0 82.4 jit_solution(10685232371482717973)
XLA Ops:
  0.0 0.9 %copy.20 = s32[1,2,32,2]{3,2,1,0:T(8,128)S(1)} copy(s32[1,2,32,2]{2,3,1,0:T(2,128)} %param.7) | data formatting | bytes 1024 | tf_op args[1]
  2.7 1.1 %multiply_reduce_fusion = f32[2,32]{1,0:T(2,128)S(1)} fusion(bf16[1,2,32,2048]{3,2,1,0:T(8,128)(2,1)} %param.6), kind=kLoop, calls=%fused_computation.21 | loop fusion | flops 393152 | bytes 262400 | tf_op jit(solution)/shard_map/reduce_sum | solution.py:30
  3.9 1.4 %convolution_convert_fusion = bf16[192,2048]{1,0:T(8,128)(2,1)S(1)} fusion(pred[64,192]{1,0:T(8,128)(4,1)S(1)} %fusion.24, bf16[64,2048]{1,0:T(8,128)(2,1)} %bitcast.57, f32[2048]{0:T(1024)} %bitcast.61, f32[64]{0:T(128)S(1)} %rsqrt.12), kind=kOutput, calls=%fused_computation.4 | convolution fusion | flops 51249152 | bytes 1069312 | tf_op jit(solution)/shard_map/tq,td->qd/dot_general | solution.py:57
  5.3 26.3 %all_to_all.5 = bf16[4,48,2048]{2,1,0:T(8,128)(2,1)S(1)} all-to-all(bf16[4,48,2048]{2,1,0:T(8,128)(2,1)S(1)} %bitcast.54), channel_id=1, replica_groups=mesh['section'=4,'z'=4,'core'=2] {'z'}, dimensions={0} | all-to-all | bytes 1572864 | tf_op jit(solution)/shard_map/all_to_all | solution.py:59
  31.5 0.9 %copy-done.1 = bf16[4,48,2048]{2,1,0:T(8,128)(2,1)} copy-done((bf16[4,48,2048]{2,1,0:T(8,128)(2,1)}, bf16[4,48,2048]{2,1,0:T(8,128)(2,1)S(1)}, u32[]{:S(2)}) %copy-start.1) | copy-done | bytes 786456
  32.4 2.3 %collective-permute-done.2 = bf16[4,48,2048]{2,1,0:T(8,128)(2,1)S(1)} collective-permute-done((bf16[4,48,2048]{2,1,0:T(8,128)(2,1)S(1)}, bf16[4,48,2048]{2,1,0:T(8,128)(2,1)S(1)}, u32[]{:S(2)}, u32[]{:S(2)}) %collective-permute-start.2) | collective-permute-done | bytes 786464 | tf_op jit(solution)/shard_map/ppermute | solution.py:17
  34.7 0.8 fusion
  36.1 1.5 %convolution_convert_fusion.1 = bf16[192,2048]{1,0:T(8,128)(2,1)} fusion(bf16[1,1,384,2048]{3,2,1,0:T(8,128)(2,1)S(1)} %copy-done.4, f32[192,768]{1,0:T(8,128)S(1)} %fusion), kind=kOutput, calls=%fused_computation.5 | convolution fusion | flops 302825472 | bytes 2949120 | tf_op jit(solution)/shard_map/dot_general | solution.py:38
  37.7 2.0 %fusion.2 = f32[192,768]{1,0:T(8,128)S(1)} fusion(bf16[192,2048]{1,0:T(8,128)(2,1)} %bitcast.55, bf16[1,1,2048,768]{3,2,1,0:T(8,128)(2,1)S(1)} %copy-done), kind=kOutput, calls=%fused_computation.2 | convolution fusion | flops 603979776 | bytes 4521984 | tf_op jit(solution)/shard_map/dot_general | solution.py:36
  40.4 1.4 %fusion.9 = bf16[4,48,2048]{2,1,0:T(8,128)(2,1)S(1)} fusion(bf16[4,48,2048]{2,1,0:T(8,128)(2,1)S(1)} %bitcast.59, bf16[4,48,2048]{2,1,0:T(8,128)(2,1)} %collective-permute-done.3), kind=kLoop, calls=%fused_computation.14 | loop fusion | flops 1572864 | bytes 2359296 | tf_op jit(solution)/shard_map/convert_element_type | solution.py:65
  41.8 1.1 %dynamic-slice_bitcast_fusion.6 = (bf16[48,2048]{1,0:T(8,128)(2,1)}, bf16[48,2048]{1,0:T(8,128)(2,1)}, bf16[48,2048]{1,0:T(8,128)(2,1)}, bf16[48,2048]{1,0:T(8,1...) fusion(bf16[4,48,2048]{2,1,0:T(8,128)(2,1)S(1)} %fusion.9, s32[]{:T(128)S(6)} %min.30, ...), kind=kLoop, calls=%fused_computation.35 | loop fusion | bytes 2752540 | tf_op jit(solution)/shard_map/jit(dynamic_index_in_dim)/squeeze | solution.py:75
  42.9 3.7 %collective-permute-start.9 = (bf16[48,2048]{1,0:T(8,128)(2,1)}, bf16[48,2048]{1,0:T(8,128)(2,1)}, u32[]{:S(2)}, u32[]{:S(2)}) collective-permute-start(bf16[48,2048]{1,0:T(8,128)(2,1)} %get-tuple-element.7), channel_id=1, source_target_pairs={{0,12},{2,14},{8,20},{10,22},{16,28},{18,30},{24,4},{26,6},{1,13},... | collective-permute-start | bytes 589832 | tf_op jit(solution)/shard_map/ppermute | solution.py:82
  46.8 1.5 %collective-permute-start.1 = (f32[64,192]{1,0:T(8,128)S(1)}, f32[64,192]{1,0:T(8,128)S(1)}, u32[]{:S(2)}, u32[]{:S(2)}) collective-permute-start(f32[64,192]{1,0:T(8,128)S(1)} %select_reduce_fusion), channel_id=1, source_target_pairs={{0,8},{8,16},{16,24},{24,0},{1,9},{9,17},{17,25},{25,1},{2,10},{10... | collective-permute-start | bytes 147464 | tf_op jit(solution)/shard_map/ppermute | solution.py:13
  48.4 1.5 %collective-permute-start = (bf16[2,32,2048]{2,1,0:T(8,128)(2,1)S(1)}, bf16[2,32,2048]{2,1,0:T(8,128)(2,1)}, u32[]{:S(2)}, u32[]{:S(2)}) collective-permute-start(bf16[2,32,2048]{2,1,0:T(8,128)(2,1)S(1)} %bitcast.58), channel_id=1, source_target_pairs={{0,8},{8,16},{16,24},{24,0},{1,9},{9,17},{17,25},{25,1},{2,10},{10... | collective-permute-start | bytes 786440 | tf_op jit(solution)/shard_map/ppermute | solution.py:13
  49.9 3.6 %collective-permute-start.8 = (bf16[48,2048]{1,0:T(8,128)(2,1)}, bf16[48,2048]{1,0:T(8,128)(2,1)S(1)}, u32[]{:S(2)}, u32[]{:S(2)}) collective-permute-start(bf16[48,2048]{1,0:T(8,128)(2,1)} %get-tuple-element.8), channel_id=1, source_target_pairs={{0,10},{2,12},{4,14},{8,18},{10,20},{12,22},{16,26},{18,28},{20,30... | collective-permute-start | bytes 589832 | tf_op jit(solution)/shard_map/ppermute | solution.py:82
  53.5 1.3 %collective-permute-start.6 = (bf16[48,2048]{1,0:T(8,128)(2,1)}, bf16[48,2048]{1,0:T(8,128)(2,1)S(1)}, u32[]{:S(2)}, u32[]{:S(2)}) collective-permute-start(bf16[48,2048]{1,0:T(8,128)(2,1)} %get-tuple-element.10), channel_id=1, source_target_pairs={{2,8},{4,10},{6,12},{10,16},{12,18},{14,20},{18,24},{20,26},{22,28... | collective-permute-start | bytes 589832 | tf_op jit(solution)/shard_map/ppermute | solution.py:82
  54.8 1.3 %collective-permute-start.5 = (bf16[48,2048]{1,0:T(8,128)(2,1)}, bf16[48,2048]{1,0:T(8,128)(2,1)S(1)}, u32[]{:S(2)}, u32[]{:S(2)}) collective-permute-start(bf16[48,2048]{1,0:T(8,128)(2,1)} %get-tuple-element.11), channel_id=1, source_target_pairs={{4,8},{6,10},{12,16},{14,18},{20,24},{22,26},{28,0},{30,2},{5,9},{... | collective-permute-start | bytes 589832 | tf_op jit(solution)/shard_map/ppermute | solution.py:82
  56.1 1.5 %collective-permute-start.7 = (bf16[48,2048]{1,0:T(8,128)(2,1)}, bf16[48,2048]{1,0:T(8,128)(2,1)S(1)}, u32[]{:S(2)}, u32[]{:S(2)}) collective-permute-start(bf16[48,2048]{1,0:T(8,128)(2,1)} %get-tuple-element.9), channel_id=1, source_target_pairs={{0,8},{2,10},{4,12},{6,14},{8,16},{10,18},{12,20},{14,22},{16,24},... | collective-permute-start | bytes 589832 | tf_op jit(solution)/shard_map/ppermute | solution.py:82
  57.7 1.3 %fusion.28 = f32[64,2048]{1,0:T(8,128)S(1)} fusion(bf16[48,2048]{1,0:T(8,128)(2,1)} %collective-permute-done.9, f32[64,192]{1,0:T(8,128)S(1)} %collective-permute-done.1, s32[]{:T(128)S(6)} %select_n.61), kind=kOutput, calls=%fused_computation.46 | convolution fusion | flops 75497472 | bytes 753668 | tf_op jit(solution)/shard_map/dot_general | solution.py:85
  59.1 9.3 %collective-permute-start.10 = (bf16[48,2048]{1,0:T(8,128)(2,1)}, bf16[48,2048]{1,0:T(8,128)(2,1)S(1)}, u32[]{:S(2)}, u32[]{:S(2)}) collective-permute-start(bf16[48,2048]{1,0:T(8,128)(2,1)} %get-tuple-element.6), channel_id=1, source_target_pairs={{0,14},{8,22},{16,30},{24,6},{1,15},{9,23},{17,31},{25,7}} | collective-permute-start | bytes 589832 | tf_op jit(solution)/shard_map/ppermute | solution.py:82
  68.8 1.3 %collective-permute-start.4 = (bf16[48,2048]{1,0:T(8,128)(2,1)}, bf16[48,2048]{1,0:T(8,128)(2,1)S(1)}, u32[]{:S(2)}, u32[]{:S(2)}) collective-permute-start(bf16[48,2048]{1,0:T(8,128)(2,1)} %get-tuple-element.5), channel_id=1, source_target_pairs={{6,8},{14,16},{22,24},{30,0},{7,9},{15,17},{23,25},{31,1}} | collective-permute-start | bytes 589832 | tf_op jit(solution)/shard_map/ppermute | solution.py:82
  70.5 3.4 %collective-permute-done.5 = bf16[48,2048]{1,0:T(8,128)(2,1)S(1)} collective-permute-done((bf16[48,2048]{1,0:T(8,128)(2,1)}, bf16[48,2048]{1,0:T(8,128)(2,1)S(1)}, u32[]{:S(2)}, u32[]{:S(2)}) %collective-permute-start.5) | collective-permute-done | bytes 196640 | tf_op jit(solution)/shard_map/ppermute | solution.py:82
  75.2 4.9 %collective-permute-done.4 = bf16[48,2048]{1,0:T(8,128)(2,1)S(1)} collective-permute-done((bf16[48,2048]{1,0:T(8,128)(2,1)}, bf16[48,2048]{1,0:T(8,128)(2,1)S(1)}, u32[]{:S(2)}, u32[]{:S(2)}) %collective-permute-start.4) | collective-permute-done | bytes 196640 | tf_op jit(solution)/shard_map/ppermute | solution.py:82
  80.7 1.7 %fusion.16 = bf16[1,2,32,2048]{3,2,1,0:T(8,128)(2,1)} fusion(f32[2,32,2048]{2,1,0:T(8,128)S(1)} %bitcast.56, bf16[2,32,2048]{2,1,0:T(8,128)(2,1)} %collective-permute-done), kind=kLoop, calls=%fused_computation.26 | loop fusion | flops 393216 | bytes 1048576 | tf_op jit(solution)/shard_map/broadcast_in_dim | solution.py:92
  (47 shorter events, 6.1 us)
Async XLA Ops:
  0.0 34.7 %copy-start = (bf16[1,1,2048,768]{3,2,1,0:T(8,128)(2,1)S(1)}, bf16[1,1,2048,768]{3,2,1,0:T(8,128)(2,1)}, u32[]{:S(2)}) copy-start(bf16[1,1,2048,768]{3,2,1,0:T(8,128)(2,1)} %param.10) | copy-start | bytes 9437188
  31.5 0.9 %copy-start.1 = (bf16[4,48,2048]{2,1,0:T(8,128)(2,1)}, bf16[4,48,2048]{2,1,0:T(8,128)(2,1)S(1)}, u32[]{:S(2)}) copy-start(bf16[4,48,2048]{2,1,0:T(8,128)(2,1)S(1)} %all_to_all.5) | copy-start | bytes 2359300
  32.4 2.3 %collective-permute-start.2 = (bf16[4,48,2048]{2,1,0:T(8,128)(2,1)S(1)}, bf16[4,48,2048]{2,1,0:T(8,128)(2,1)S(1)}, u32[]{:S(2)}, u32[]{:S(2)}) collective-permute-start(bf16[4,48,2048]{2,1,0:T(8,128)(2,1)S(1)} %all_to_all.5), channel_id=1, source_target_pairs={{0,1},{1,0},{2,3},{3,2},{4,5},{5,4},{6,7},{7,6},{8,9},{9,8},{10,11... | collective-permute-start | bytes 2359304 | tf_op jit(solution)/shard_map/ppermute | solution.py:17
  34.7 1.4 %copy-start.4 = (bf16[1,1,384,2048]{3,2,1,0:T(8,128)(2,1)S(1)}, bf16[1,1,384,2048]{3,2,1,0:T(8,128)(2,1)}, u32[]{:S(2)}) copy-start(bf16[1,1,384,2048]{3,2,1,0:T(8,128)(2,1)} %param.11) | copy-start | bytes 4718596
  37.6 2.8 %collective-permute-start.3 = (bf16[4,48,2048]{2,1,0:T(8,128)(2,1)}, bf16[4,48,2048]{2,1,0:T(8,128)(2,1)}, u32[]{:S(2)}, u32[]{:S(2)}) collective-permute-start(bf16[4,48,2048]{2,1,0:T(8,128)(2,1)} %bitcast.9), channel_id=1, source_target_pairs={{0,1},{1,0},{2,3},{3,2},{4,5},{5,4},{6,7},{7,6},{8,9},{9,8},{10,11... | collective-permute-start | bytes 2359304 | tf_op jit(solution)/shard_map/ppermute | solution.py:17
  37.7 2.0 %copy-start.5 = (bf16[1,1,384,2048]{3,2,1,0:T(8,128)(2,1)S(1)}, bf16[1,1,384,2048]{3,2,1,0:T(8,128)(2,1)}, u32[]{:S(2)}) copy-start(bf16[1,1,384,2048]{3,2,1,0:T(8,128)(2,1)} %param.11) | copy-start | bytes 4718596
  41.8 4.8 %copy-start.3 = (f32[1,2,32,2]{2,3,1,0:T(2,128)S(1)}, f32[1,2,32,2]{2,3,1,0:T(2,128)}, u32[]{:S(2)}) copy-start(f32[1,2,32,2]{2,3,1,0:T(2,128)} %param.8) | copy-start | bytes 1540
  41.8 6.6 %copy-start.2 = (bf16[1,2,32,2048]{3,2,1,0:T(8,128)(2,1)S(1)}, bf16[1,2,32,2048]{3,2,1,0:T(8,128)(2,1)}, u32[]{:S(2)}) copy-start(bf16[1,2,32,2048]{3,2,1,0:T(8,128)(2,1)} %param.6) | copy-start | bytes 786436
  42.9 13.2 %collective-permute-start.9 = (bf16[48,2048]{1,0:T(8,128)(2,1)}, bf16[48,2048]{1,0:T(8,128)(2,1)}, u32[]{:S(2)}, u32[]{:S(2)}) collective-permute-start(bf16[48,2048]{1,0:T(8,128)(2,1)} %get-tuple-element.7), channel_id=1, source_target_pairs={{0,12},{2,14},{8,20},{10,22},{16,28},{18,30},{24,4},{26,6},{1,13},... | collective-permute-start | bytes 589832 | tf_op jit(solution)/shard_map/ppermute | solution.py:82
  46.8 8.0 %collective-permute-start.1 = (f32[64,192]{1,0:T(8,128)S(1)}, f32[64,192]{1,0:T(8,128)S(1)}, u32[]{:S(2)}, u32[]{:S(2)}) collective-permute-start(f32[64,192]{1,0:T(8,128)S(1)} %select_reduce_fusion), channel_id=1, source_target_pairs={{0,8},{8,16},{16,24},{24,0},{1,9},{9,17},{17,25},{25,1},{2,10},{10... | collective-permute-start | bytes 147464 | tf_op jit(solution)/shard_map/ppermute | solution.py:13
  48.4 32.3 %collective-permute-start = (bf16[2,32,2048]{2,1,0:T(8,128)(2,1)S(1)}, bf16[2,32,2048]{2,1,0:T(8,128)(2,1)}, u32[]{:S(2)}, u32[]{:S(2)}) collective-permute-start(bf16[2,32,2048]{2,1,0:T(8,128)(2,1)S(1)} %bitcast.58), channel_id=1, source_target_pairs={{0,8},{8,16},{16,24},{24,0},{1,9},{9,17},{17,25},{25,1},{2,10},{10... | collective-permute-start | bytes 786440 | tf_op jit(solution)/shard_map/ppermute | solution.py:13
  49.9 9.2 %collective-permute-start.8 = (bf16[48,2048]{1,0:T(8,128)(2,1)}, bf16[48,2048]{1,0:T(8,128)(2,1)S(1)}, u32[]{:S(2)}, u32[]{:S(2)}) collective-permute-start(bf16[48,2048]{1,0:T(8,128)(2,1)} %get-tuple-element.8), channel_id=1, source_target_pairs={{0,10},{2,12},{4,14},{8,18},{10,20},{12,22},{16,26},{18,28},{20,30... | collective-permute-start | bytes 589832 | tf_op jit(solution)/shard_map/ppermute | solution.py:82
  53.5 15.3 %collective-permute-start.6 = (bf16[48,2048]{1,0:T(8,128)(2,1)}, bf16[48,2048]{1,0:T(8,128)(2,1)S(1)}, u32[]{:S(2)}, u32[]{:S(2)}) collective-permute-start(bf16[48,2048]{1,0:T(8,128)(2,1)} %get-tuple-element.10), channel_id=1, source_target_pairs={{2,8},{4,10},{6,12},{10,16},{12,18},{14,20},{18,24},{20,26},{22,28... | collective-permute-start | bytes 589832 | tf_op jit(solution)/shard_map/ppermute | solution.py:82
  54.8 19.1 %collective-permute-start.5 = (bf16[48,2048]{1,0:T(8,128)(2,1)}, bf16[48,2048]{1,0:T(8,128)(2,1)S(1)}, u32[]{:S(2)}, u32[]{:S(2)}) collective-permute-start(bf16[48,2048]{1,0:T(8,128)(2,1)} %get-tuple-element.11), channel_id=1, source_target_pairs={{4,8},{6,10},{12,16},{14,18},{20,24},{22,26},{28,0},{30,2},{5,9},{... | collective-permute-start | bytes 589832 | tf_op jit(solution)/shard_map/ppermute | solution.py:82
  56.1 18.2 %collective-permute-start.7 = (bf16[48,2048]{1,0:T(8,128)(2,1)}, bf16[48,2048]{1,0:T(8,128)(2,1)S(1)}, u32[]{:S(2)}, u32[]{:S(2)}) collective-permute-start(bf16[48,2048]{1,0:T(8,128)(2,1)} %get-tuple-element.9), channel_id=1, source_target_pairs={{0,8},{2,10},{4,12},{6,14},{8,16},{10,18},{12,20},{14,22},{16,24},... | collective-permute-start | bytes 589832 | tf_op jit(solution)/shard_map/ppermute | solution.py:82
  59.1 15.7 %collective-permute-start.10 = (bf16[48,2048]{1,0:T(8,128)(2,1)}, bf16[48,2048]{1,0:T(8,128)(2,1)S(1)}, u32[]{:S(2)}, u32[]{:S(2)}) collective-permute-start(bf16[48,2048]{1,0:T(8,128)(2,1)} %get-tuple-element.6), channel_id=1, source_target_pairs={{0,14},{8,22},{16,30},{24,6},{1,15},{9,23},{17,31},{25,7}} | collective-permute-start | bytes 589832 | tf_op jit(solution)/shard_map/ppermute | solution.py:82
  68.8 11.4 %collective-permute-start.4 = (bf16[48,2048]{1,0:T(8,128)(2,1)}, bf16[48,2048]{1,0:T(8,128)(2,1)S(1)}, u32[]{:S(2)}, u32[]{:S(2)}) collective-permute-start(bf16[48,2048]{1,0:T(8,128)(2,1)} %get-tuple-element.5), channel_id=1, source_target_pairs={{6,8},{14,16},{22,24},{30,0},{7,9},{15,17},{23,25},{31,1}} | collective-permute-start | bytes 589832 | tf_op jit(solution)/shard_map/ppermute | solution.py:82

commit v7 on v5

--- a/solution.py
+++ b/solution.py
@@ -39,33 +39,22 @@
     return partial_out.astype(jnp.bfloat16)
 
 
-def local(tokens, routes, combine_weights, norm_gain, gate_up, down):
-    inputs = tokens[0]
-    micro, tok_count, width = inputs.shape
-    experts = lax.axis_size("z")
-    topk = routes.shape[3]
-    capacity = 2 * ((3 * tok_count * topk + 4 * experts - 1) // (4 * experts))
-    block = micro * capacity
-    normed = normalize(inputs, norm_gain[0]).reshape(-1, width)
-    codes = jax.vmap(lambda one: slot_codes(one, experts, capacity))(routes[0])
-    chosen = codes // capacity
-    place = chosen * block + jnp.arange(micro, dtype=jnp.int32)[:, None, None] * capacity
-    place = (place + codes % capacity).reshape(micro * tok_count, topk)
-    lanes = jnp.arange(experts * block, dtype=jnp.int32)
-    hits = place[..., None] == lanes
+def one_micro(inputs, normed, codes, weights, gate_up, down, experts, capacity):
+    width = inputs.shape[-1]
+    lanes = jnp.arange(experts * capacity, dtype=jnp.int32)
+    hits = codes[..., None] == lanes
     onehot = jnp.any(hits, axis=1).astype(jnp.bfloat16)
     buffer = jnp.einsum("tq,td->qd", onehot, normed, preferred_element_type=jnp.float32)
-    buffer = buffer.astype(jnp.bfloat16).reshape(experts, block, width)
+    buffer = buffer.astype(jnp.bfloat16).reshape(experts, capacity, width)
     incoming = lax.all_to_all(buffer, "z", split_axis=0, concat_axis=0, tiled=True)
     partner_rows = swap_cores(incoming)
-    own = expert_half(incoming.reshape(-1, width), gate_up[0, 0], down[0, 0])
-    lent = expert_half(partner_rows.reshape(-1, width), gate_up[0, 0], down[0, 0])
+    own = expert_half(incoming.reshape(-1, width), gate_up, down)
+    lent = expert_half(partner_rows.reshape(-1, width), gate_up, down)
     other_half = swap_cores(lent.reshape(incoming.shape))
     results = (own.reshape(incoming.shape).astype(jnp.float32) + other_half.astype(jnp.float32))
     results = results.astype(jnp.bfloat16)
     returned = lax.all_to_all(results, "z", split_axis=0, concat_axis=0, tiled=True)
     table = returned.reshape(-1, width)
-    weights = combine_weights[0].reshape(micro * tok_count, topk)
     mixing = jnp.sum(jnp.where(hits, weights[..., None], 0.0), axis=1)
     combined = jnp.dot(
         mixing,
@@ -73,9 +62,32 @@
         precision=lax.Precision.HIGHEST,
         preferred_element_type=jnp.float32,
     )
-    mixed = inputs.astype(jnp.float32) + combined.reshape(micro, tok_count, width)
-    moved = from_behind(mixed.astype(jnp.bfloat16), "section", 1)
-    return moved[None]
+    mixed = inputs.astype(jnp.float32) + combined
+    return from_behind(mixed.astype(jnp.bfloat16), "section", 1)
+
+
+def local(tokens, routes, combine_weights, norm_gain, gate_up, down):
+    inputs = tokens[0]
+    micro, tok_count, width = inputs.shape
+    experts = lax.axis_size("z")
+    topk = routes.shape[3]
+    capacity = 2 * ((3 * tok_count * topk + 4 * experts - 1) // (4 * experts))
+    normed = normalize(inputs, norm_gain[0])
+    codes = jax.vmap(lambda one: slot_codes(one, experts, capacity))(routes[0])
+    pieces = [
+        one_micro(
+            inputs[m],
+            normed[m],
+            codes[m],
+            combine_weights[0, m],
+            gate_up[0, 0],
+            down[0, 0],
+            experts,
+            capacity,
+        )
+        for m in range(micro)
+    ]
+    return jnp.stack(pieces)[None]
 
 
 def solution(mesh):

time: 75.6 us -> 88.9 us (1.18)
  blocking collectives: 26.3 us -> 0 us
  starting transfers between devices: 5.93 us -> 22.4 us
  matrix products: 4.81 us -> 16.3 us
  waiting for transfers between devices: 30.5 us -> 37.6 us
  other arithmetic: 4.68 us -> 6.99 us
  local copies, waits for them, and re-layouts: 2.94 us -> 4.62 us
    all_to_all x1 -> x0, blocking collectives: 26.3 us -> none  [local(): lax.all_to_all(buffer, 'z', split_axis=0, concat_axis=0, tiled=True)]
    all_to_all x1 -> x4, starting transfers between devices: 4.19 us -> 18.7 us  [the longest x2 10.5 us: one_micro(): lax.all_to_all(buffer, 'z', split_axis=0, concat_axis=0, tiled=True)]
    all_to_all x1 -> x4, waiting for transfers between devices: 20.5 us -> 33.2 us  [the longest x2 16.9 us: one_micro(): lax.all_to_all(results, 'z', split_axis=0, concat_axis=0, tiled=True)]
    dot_general x2 -> x4, matrix products: 2.07 us -> 6.22 us  [the longest x2 3.22 us: one_micro(): jnp.dot(mixing, table.astype(jnp.float32), precision=lax.Precision.HIGHES...]
    dot_general x2 -> x4, matrix products: 1.55 us -> 5.32 us  [expert_half(): joined = jnp.dot(token_rows, weights_gu, preferred_element_type=jnp.float32)]
    dot_general x2 -> x4, matrix products: 1.19 us -> 4.8 us  [expert_half(): jnp.dot(hidden, weights_dn, preferred_element_type=jnp.float32)]
    ppermute x2 -> x4, waiting for transfers between devices: 3.05 us -> 0.01 us  [swap_cores(): return lax.ppermute(value, 'core', [(0, 1), (1, 0)])]
    ppermute x1 -> x2, waiting for transfers between devices: 6.9 us -> 4.38 us  [from_behind(): return lax.ppermute(value, axis, pairs)]
  transfers between devices with their start and end apart: 4 -> 10, of which waited for: 4 -> 5; matrix products, arithmetic and copies ran while one was open for 2% -> 23% of each run, Pallas kernels for 0% -> 0%
where the time goes in v7:
time: 88.9 us; the launch traced here: 88.2 us
  waiting for transfers between devices  37.6 us (42%)
  starting transfers between devices  22.4 us (25%)
  matrix products  16.3 us (18%)
  other arithmetic  6.99 us (8%)
  local copies, waits for them, and re-layouts  4.62 us (5%)
    all_to_all x2, waiting for transfers between devices, one_micro(): lax.all_to_all(results, 'z', split_axis=0, concat_axis=0, tiled=True)  16.9 us
    all_to_all x2, waiting for transfers between devices, one_micro(): lax.all_to_all(buffer, 'z', split_axis=0, concat_axis=0, tiled=True)  16.3 us
    all_to_all x2, starting transfers between devices, one_micro(): lax.all_to_all(buffer, 'z', split_axis=0, concat_axis=0, tiled=True)  10.5 us
    all_to_all x2, starting transfers between devices, one_micro(): lax.all_to_all(results, 'z', split_axis=0, concat_axis=0, tiled=True)  8.2 us
    dot_general x4, matrix products, expert_half(): joined = jnp.dot(token_rows, weights_gu, preferred_element_type=jnp.float32)  5.32 us
    dot_general x4, matrix products, expert_half(): jnp.dot(hidden, weights_dn, preferred_element_type=jnp.float32)  4.8 us
    ppermute x2, waiting for transfers between devices, from_behind(): return lax.ppermute(value, axis, pairs)  4.38 us
    dot_general x2, matrix products, one_micro(): jnp.dot(mixing, table.astype(jnp.float32), precision=lax.Precision.HIGHES...  3.22 us
  transfers between devices with their start and end apart: 10, of which 5 were waited for; matrix products, arithmetic and copies ran while one was open for 23% of the time, Pallas kernels for 0%

profile of v7, /device:TPU:0, one launch (start us, length us, event | category | flops | bytes accessed | tf_op | source)
XLA Modules:
  0.0 88.2 jit_solution(15479860405566977766)
XLA Ops:
  0.0 0.9 %copy.13 = s32[1,2,32,2]{3,2,1,0:T(8,128)S(1)} copy(s32[1,2,32,2]{2,3,1,0:T(2,128)} %param.7) | data formatting | bytes 1024 | tf_op args[1]
  2.3 1.1 %fusion.16 = f32[2,32]{1,0:T(2,128)S(1)} fusion(bf16[1,2,32,2048]{3,2,1,0:T(8,128)(2,1)} %param.6), kind=kLoop, calls=%fused_computation.28 | loop fusion | flops 393152 | bytes 262400 | tf_op jit(solution)/shard_map/reduce_sum | solution.py:30
  3.4 1.1 %fusion.18 = bf16[2,32,2048]{2,1,0:T(8,128)(2,1)S(1)} fusion(bf16[1,2,32,2048]{3,2,1,0:T(8,128)(2,1)} %param.6, f32[2048]{0:T(1024)} %bitcast.78, f32[2,32]{1,0:T(2,128)S(1)} %add_rsqrt_fusion), kind=kLoop, calls=%fused_computation.30 | loop fusion | flops 524288 | bytes 532736 | tf_op jit(solution)/shard_map/convert_element_type | solution.py:31
  5.2 1.0 %convolution_convert_fusion.5 = bf16[96,2048]{1,0:T(8,128)(2,1)} fusion(pred[32,96]{1,0:T(8,128)(4,1)S(1)} %fusion.33, bf16[2,32,2048]{2,1,0:T(8,128)(2,1)S(1)} %fusion.18), kind=kOutput, calls=%fused_computation.13 | convolution fusion | flops 12779520 | bytes 528384 | tf_op jit(solution)/shard_map/tq,td->qd/dot_general | solution.py:47
  6.2 6.3 %all-to-all-start = ((bf16[4,24,2048]{2,1,0:T(8,128)(2,1)}), bf16[4,24,2048]{2,1,0:T(8,128)(2,1)S(1)}, u32[]{:S(2)}, u32[]{:S(2)}) async-start(bf16[4,24,2048]{2,1,0:T(8,128)(2,1)} %bitcast.72), calls=%async_computation | async-start | bytes 786432 | tf_op jit(solution)/shard_map/all_to_all | solution.py:49
  14.7 2.0 %convolution_convert_fusion.2 = bf16[96,2048]{1,0:T(8,128)(2,1)} fusion(pred[32,96]{1,0:T(8,128)(4,1)S(1)} %fusion.32, bf16[2,32,2048]{2,1,0:T(8,128)(2,1)} %copy-done.5), kind=kOutput, calls=%fused_computation.10 | convolution fusion | flops 12779520 | bytes 527360 | tf_op jit(solution)/shard_map/tq,td->qd/dot_general | solution.py:47
  16.7 7.6 %all-to-all-done = bf16[4,24,2048]{2,1,0:T(8,128)(2,1)S(1)} async-done(((bf16[4,24,2048]{2,1,0:T(8,128)(2,1)}), bf16[4,24,2048]{2,1,0:T(8,128)(2,1)S(1)}, u32[]{:S(2)}, u32[]{:S(2)}) %all-to-all-start) | async-done | bytes 393248 | tf_op jit(solution)/shard_map/all_to_all | solution.py:49
  24.3 4.1 %all-to-all-start.2 = ((bf16[4,24,2048]{2,1,0:T(8,128)(2,1)}), bf16[4,24,2048]{2,1,0:T(8,128)(2,1)}, u32[]{:S(2)}, u32[]{:S(2)}) async-start(bf16[4,24,2048]{2,1,0:T(8,128)(2,1)} %bitcast.71), calls=%async_computation.2 | async-start | bytes 786432 | tf_op jit(solution)/shard_map/all_to_all | solution.py:49
  29.8 1.2 %convolution_convert_fusion.4 = bf16[96,2048]{1,0:T(8,128)(2,1)} fusion(bf16[1,1,384,2048]{3,2,1,0:T(8,128)(2,1)S(1)} %copy-done.1, f32[96,768]{1,0:T(8,128)S(1)} %fusion.6), kind=kOutput, calls=%fused_computation.12 | convolution fusion | flops 151412736 | bytes 2260992 | tf_op jit(solution)/shard_map/dot_general | solution.py:38
  31.0 8.7 %all-to-all-done.2 = bf16[4,24,2048]{2,1,0:T(8,128)(2,1)} async-done(((bf16[4,24,2048]{2,1,0:T(8,128)(2,1)}), bf16[4,24,2048]{2,1,0:T(8,128)(2,1)}, u32[]{:S(2)}, u32[]{:S(2)}) %all-to-all-start.2) | async-done | bytes 393248 | tf_op jit(solution)/shard_map/all_to_all | solution.py:49
  39.7 2.5 %fusion.2 = f32[96,768]{1,0:T(8,128)} fusion(bf16[96,2048]{1,0:T(8,128)(2,1)} %bitcast.19, bf16[1,1,2048,768]{3,2,1,0:T(8,128)(2,1)S(1)} %copy-done), kind=kOutput, calls=%fused_computation.2 | convolution fusion | flops 301989888 | bytes 3833856 | tf_op jit(solution)/shard_map/dot_general | solution.py:36
  42.1 1.6 %fusion.4 = f32[96,768]{1,0:T(8,128)S(1)} fusion(bf16[96,2048]{1,0:T(8,128)(2,1)} %bitcast.11, bf16[1,1,2048,768]{3,2,1,0:T(8,128)(2,1)S(1)} %copy-done), kind=kOutput, calls=%fused_computation.4 | convolution fusion | flops 301989888 | bytes 3833856 | tf_op jit(solution)/shard_map/dot_general | solution.py:36
  45.4 1.2 %convolution_convert_fusion = bf16[96,2048]{1,0:T(8,128)(2,1)} fusion(bf16[1,1,384,2048]{3,2,1,0:T(8,128)(2,1)S(1)} %copy-done.2, f32[96,768]{1,0:T(8,128)S(1)} %fusion), kind=kOutput, calls=%fused_computation.8 | convolution fusion | flops 151412736 | bytes 2260992 | tf_op jit(solution)/shard_map/dot_general | solution.py:38
  47.6 4.1 %all-to-all-start.1 = ((bf16[4,24,2048]{2,1,0:T(8,128)(2,1)}), bf16[4,24,2048]{2,1,0:T(8,128)(2,1)}, u32[]{:S(2)}, u32[]{:S(2)}) async-start(bf16[4,24,2048]{2,1,0:T(8,128)(2,1)} %fusion.15), calls=%async_computation.1 | async-start | bytes 786432 | tf_op jit(solution)/shard_map/all_to_all | solution.py:56
  51.7 2.0 %convolution_convert_fusion.1 = bf16[96,2048]{1,0:T(8,128)(2,1)S(1)} fusion(bf16[1,1,384,2048]{3,2,1,0:T(8,128)(2,1)} %param.11, f32[96,768]{1,0:T(8,128)} %fusion.2), kind=kOutput, calls=%fused_computation.9 | convolution fusion | flops 151412736 | bytes 2260992 | tf_op jit(solution)/shard_map/dot_general | solution.py:38
  53.7 1.8 %fusion.14 = bf16[4,24,2048]{2,1,0:T(8,128)(2,1)} fusion(bf16[4,24,2048]{2,1,0:T(8,128)(2,1)S(1)} %bitcast.73, bf16[4,24,2048]{2,1,0:T(8,128)(2,1)} %collective-permute-done.4), kind=kLoop, calls=%fused_computation.23 | loop fusion | flops 786432 | bytes 1179648 | tf_op jit(solution)/shard_map/convert_element_type | solution.py:55
  55.6 8.8 %all-to-all-done.1 = bf16[4,24,2048]{2,1,0:T(8,128)(2,1)} async-done(((bf16[4,24,2048]{2,1,0:T(8,128)(2,1)}), bf16[4,24,2048]{2,1,0:T(8,128)(2,1)}, u32[]{:S(2)}, u32[]{:S(2)}) %all-to-all-start.1) | async-done | bytes 393248 | tf_op jit(solution)/shard_map/all_to_all | solution.py:56
  64.4 4.1 %all-to-all-start.3 = ((bf16[4,24,2048]{2,1,0:T(8,128)(2,1)}), bf16[4,24,2048]{2,1,0:T(8,128)(2,1)}, u32[]{:S(2)}, u32[]{:S(2)}) async-start(bf16[4,24,2048]{2,1,0:T(8,128)(2,1)} %fusion.14), calls=%async_computation.3 | async-start | bytes 786432 | tf_op jit(solution)/shard_map/all_to_all | solution.py:56
  68.7 1.9 %fusion.8 = bf16[32,2048]{1,0:T(8,128)(2,1)} fusion(f32[32,96]{1,0:T(8,128)S(1)} %select_reduce_fusion.2, bf16[96,2048]{1,0:T(8,128)(2,1)} %bitcast.13, bf16[1,2,32,2048]{3,2,1,0:T(8,128)(2,1)S(1)} %copy-done.3), kind=kOutput, calls=%fused_computation.16 | convolution fusion | flops 75694080 | bytes 667648 | tf_op jit(solution)/shard_map/dot_general | solution.py:59
  70.7 1.5 %collective-permute-start.2 = (bf16[32,2048]{1,0:T(8,128)(2,1)}, bf16[32,2048]{1,0:T(8,128)(2,1)S(1)}, u32[]{:S(2)}, u32[]{:S(2)}) collective-permute-start(bf16[32,2048]{1,0:T(8,128)(2,1)} %fusion.8), channel_id=1, source_target_pairs={{0,8},{8,16},{16,24},{24,0},{1,9},{9,17},{17,25},{25,1},{2,10},{10... | collective-permute-start | bytes 393224 | tf_op jit(solution)/shard_map/ppermute | solution.py:13
  72.1 8.1 %all-to-all-done.3 = bf16[4,24,2048]{2,1,0:T(8,128)(2,1)} async-done(((bf16[4,24,2048]{2,1,0:T(8,128)(2,1)}), bf16[4,24,2048]{2,1,0:T(8,128)(2,1)}, u32[]{:S(2)}, u32[]{:S(2)}) %all-to-all-start.3) | async-done | bytes 393248 | tf_op jit(solution)/shard_map/all_to_all | solution.py:56
  80.3 1.3 %fusion.9 = bf16[32,2048]{1,0:T(8,128)(2,1)S(1)} fusion(f32[32,96]{1,0:T(8,128)S(1)} %select_reduce_fusion.1, bf16[96,2048]{1,0:T(8,128)(2,1)} %bitcast.23, bf16[1,2,32,2048]{3,2,1,0:T(8,128)(2,1)S(1)} %copy-done.3), kind=kOutput, calls=%fused_computation.17 | convolution fusion | flops 75694080 | bytes 667648 | tf_op jit(solution)/shard_map/dot_general | solution.py:59
  81.6 1.5 %collective-permute-start.5 = (bf16[32,2048]{1,0:T(8,128)(2,1)S(1)}, bf16[32,2048]{1,0:T(8,128)(2,1)S(1)}, u32[]{:S(2)}, u32[]{:S(2)}) collective-permute-start(bf16[32,2048]{1,0:T(8,128)(2,1)S(1)} %fusion.9), channel_id=1, source_target_pairs={{0,8},{8,16},{16,24},{24,0},{1,9},{9,17},{17,25},{25,1},{2,10},{10... | collective-permute-start | bytes 393224 | tf_op jit(solution)/shard_map/ppermute | solution.py:13
  83.1 4.4 %collective-permute-done.5 = bf16[32,2048]{1,0:T(8,128)(2,1)S(1)} collective-permute-done((bf16[32,2048]{1,0:T(8,128)(2,1)S(1)}, bf16[32,2048]{1,0:T(8,128)(2,1)S(1)}, u32[]{:S(2)}, u32[]{:S(2)}) %collective-permute-start.5) | collective-permute-done | bytes 131104 | tf_op jit(solution)/shard_map/ppermute | solution.py:13
  (50 shorter events, 9.1 us)
Async XLA Ops:
  0.0 28.5 %copy-start = (bf16[1,1,2048,768]{3,2,1,0:T(8,128)(2,1)S(1)}, bf16[1,1,2048,768]{3,2,1,0:T(8,128)(2,1)}, u32[]{:S(2)}) copy-start(bf16[1,1,2048,768]{3,2,1,0:T(8,128)(2,1)} %param.10) | copy-start | bytes 9437188
  2.2 4.0 %copy-start.6 = (s32[32,2]{0,1:T(2,128)}, s32[32,2]{0,1:T(2,128)S(1)}, u32[]{:S(2)}) copy-start(s32[32,2]{0,1:T(2,128)S(1)} %copy.14) | copy-start | bytes 772
  4.5 0.7 copy-start.5
  6.2 18.0 %all-to-all-start = ((bf16[4,24,2048]{2,1,0:T(8,128)(2,1)}), bf16[4,24,2048]{2,1,0:T(8,128)(2,1)S(1)}, u32[]{:S(2)}, u32[]{:S(2)}) async-start(bf16[4,24,2048]{2,1,0:T(8,128)(2,1)} %bitcast.72), calls=%async_computation | async-start | bytes 786432 | tf_op jit(solution)/shard_map/all_to_all | solution.py:49
  24.3 15.4 %all-to-all-start.2 = ((bf16[4,24,2048]{2,1,0:T(8,128)(2,1)}), bf16[4,24,2048]{2,1,0:T(8,128)(2,1)}, u32[]{:S(2)}, u32[]{:S(2)}) async-start(bf16[4,24,2048]{2,1,0:T(8,128)(2,1)} %bitcast.71), calls=%async_computation.2 | async-start | bytes 786432 | tf_op jit(solution)/shard_map/all_to_all | solution.py:49
  28.4 1.4 %copy-start.1 = (bf16[1,1,384,2048]{3,2,1,0:T(8,128)(2,1)S(1)}, bf16[1,1,384,2048]{3,2,1,0:T(8,128)(2,1)}, u32[]{:S(2)}) copy-start(bf16[1,1,384,2048]{3,2,1,0:T(8,128)(2,1)} %param.11) | copy-start | bytes 4718596
  28.4 13.8 %collective-permute-start = (bf16[4,24,2048]{2,1,0:T(8,128)(2,1)S(1)}, bf16[4,24,2048]{2,1,0:T(8,128)(2,1)}, u32[]{:S(2)}, u32[]{:S(2)}) collective-permute-start(bf16[4,24,2048]{2,1,0:T(8,128)(2,1)S(1)} %all-to-all-done), channel_id=1, source_target_pairs={{0,1},{1,0},{2,3},{3,2},{4,5},{5,4},{6,7},{7,6},{8,9},{9,8},{10,11... | collective-permute-start | bytes 1179656 | tf_op jit(solution)/shard_map/ppermute | solution.py:17
  39.7 5.1 %collective-permute-start.3 = (bf16[4,24,2048]{2,1,0:T(8,128)(2,1)}, bf16[4,24,2048]{2,1,0:T(8,128)(2,1)S(1)}, u32[]{:S(2)}, u32[]{:S(2)}) collective-permute-start(bf16[4,24,2048]{2,1,0:T(8,128)(2,1)} %all-to-all-done.2), channel_id=1, source_target_pairs={{0,1},{1,0},{2,3},{3,2},{4,5},{5,4},{6,7},{7,6},{8,9},{9,8},{10,11... | collective-permute-start | bytes 1179656 | tf_op jit(solution)/shard_map/ppermute | solution.py:17
  39.7 4.1 %copy-start.2 = (bf16[1,1,384,2048]{3,2,1,0:T(8,128)(2,1)S(1)}, bf16[1,1,384,2048]{3,2,1,0:T(8,128)(2,1)}, u32[]{:S(2)}) copy-start(bf16[1,1,384,2048]{3,2,1,0:T(8,128)(2,1)} %param.11) | copy-start | bytes 4718596
  44.2 2.5 %copy-start.4 = (bf16[96,2048]{1,0:T(8,128)(2,1)S(1)}, bf16[96,2048]{1,0:T(8,128)(2,1)}, u32[]{:S(2)}) copy-start(bf16[96,2048]{1,0:T(8,128)(2,1)} %convolution_convert_fusion.4) | copy-start | bytes 1179652
  44.2 2.5 %collective-permute-start.1 = (bf16[4,24,2048]{2,1,0:T(8,128)(2,1)S(1)}, bf16[4,24,2048]{2,1,0:T(8,128)(2,1)S(1)}, u32[]{:S(2)}, u32[]{:S(2)}) collective-permute-start(bf16[4,24,2048]{2,1,0:T(8,128)(2,1)S(1)} %bitcast.75), channel_id=1, source_target_pairs={{0,1},{1,0},{2,3},{3,2},{4,5},{5,4},{6,7},{7,6},{8,9},{9,8},{10,11... | collective-permute-start | bytes 1179656 | tf_op jit(solution)/shard_map/ppermute | solution.py:17
  46.6 21.9 %copy-start.9 = (f32[1,2,32,2]{2,3,1,0:T(2,128)S(1)}, f32[1,2,32,2]{2,3,1,0:T(2,128)}, u32[]{:S(2)}) copy-start(f32[1,2,32,2]{2,3,1,0:T(2,128)} %param.8) | copy-start | bytes 1540
  46.6 21.9 %copy-start.7 = (s32[32,2]{0,1:T(2,128)S(1)}, s32[32,2]{0,1:T(2,128)}, u32[]{:S(2)}) copy-start(s32[32,2]{0,1:T(2,128)} %copy-done.6) | copy-start | bytes 772
  46.6 22.0 %copy-start.8 = (s32[32,2]{0,1:T(2,128)S(1)}, s32[32,2]{0,1:T(2,128)}, u32[]{:S(2)}) copy-start(s32[32,2]{0,1:T(2,128)} %copy.15) | copy-start | bytes 772
  46.6 22.1 %copy-start.3 = (bf16[1,2,32,2048]{3,2,1,0:T(8,128)(2,1)S(1)}, bf16[1,2,32,2048]{3,2,1,0:T(8,128)(2,1)}, u32[]{:S(2)}) copy-start(bf16[1,2,32,2048]{3,2,1,0:T(8,128)(2,1)} %param.6) | copy-start | bytes 786436
  46.6 7.1 %collective-permute-start.4 = (bf16[4,24,2048]{2,1,0:T(8,128)(2,1)}, bf16[4,24,2048]{2,1,0:T(8,128)(2,1)}, u32[]{:S(2)}, u32[]{:S(2)}) collective-permute-start(bf16[4,24,2048]{2,1,0:T(8,128)(2,1)} %bitcast.22), channel_id=1, source_target_pairs={{0,1},{1,0},{2,3},{3,2},{4,5},{5,4},{6,7},{7,6},{8,9},{9,8},{10,11... | collective-permute-start | bytes 1179656 | tf_op jit(solution)/shard_map/ppermute | solution.py:17
  47.6 16.8 %all-to-all-start.1 = ((bf16[4,24,2048]{2,1,0:T(8,128)(2,1)}), bf16[4,24,2048]{2,1,0:T(8,128)(2,1)}, u32[]{:S(2)}, u32[]{:S(2)}) async-start(bf16[4,24,2048]{2,1,0:T(8,128)(2,1)} %fusion.15), calls=%async_computation.1 | async-start | bytes 786432 | tf_op jit(solution)/shard_map/all_to_all | solution.py:56
  64.4 15.9 %all-to-all-start.3 = ((bf16[4,24,2048]{2,1,0:T(8,128)(2,1)}), bf16[4,24,2048]{2,1,0:T(8,128)(2,1)}, u32[]{:S(2)}, u32[]{:S(2)}) async-start(bf16[4,24,2048]{2,1,0:T(8,128)(2,1)} %fusion.14), calls=%async_computation.3 | async-start | bytes 786432 | tf_op jit(solution)/shard_map/all_to_all | solution.py:56
  70.7 12.5 %collective-permute-start.2 = (bf16[32,2048]{1,0:T(8,128)(2,1)}, bf16[32,2048]{1,0:T(8,128)(2,1)S(1)}, u32[]{:S(2)}, u32[]{:S(2)}) collective-permute-start(bf16[32,2048]{1,0:T(8,128)(2,1)} %fusion.8), channel_id=1, source_target_pairs={{0,8},{8,16},{16,24},{24,0},{1,9},{9,17},{17,25},{25,1},{2,10},{10... | collective-permute-start | bytes 393224 | tf_op jit(solution)/shard_map/ppermute | solution.py:13
  81.6 5.9 %collective-permute-start.5 = (bf16[32,2048]{1,0:T(8,128)(2,1)S(1)}, bf16[32,2048]{1,0:T(8,128)(2,1)S(1)}, u32[]{:S(2)}, u32[]{:S(2)}) collective-permute-start(bf16[32,2048]{1,0:T(8,128)(2,1)S(1)} %fusion.9), channel_id=1, source_target_pairs={{0,8},{8,16},{16,24},{24,0},{1,9},{9,17},{17,25},{25,1},{2,10},{10... | collective-permute-start | bytes 393224 | tf_op jit(solution)/shard_map/ppermute | solution.py:13

commit v8 on v5

--- a/solution.py
+++ b/solution.py
@@ -19,9 +19,12 @@
 
 def slot_codes(route_block, experts, capacity):
     flat = route_block.reshape(-1)
-    onehot = (flat[:, None] == jnp.arange(experts, dtype=jnp.int32)[None, :]).astype(jnp.int32)
-    before = jnp.cumsum(onehot, axis=0) - onehot
-    slot = jnp.sum(before * onehot, axis=1)
+    count = flat.shape[0]
+    onehot = (flat[:, None] == jnp.arange(experts, dtype=flat.dtype)[None, :]).astype(jnp.bfloat16)
+    order = jnp.arange(count, dtype=jnp.int32)
+    earlier = (order[:, None] > order[None, :]).astype(jnp.bfloat16)
+    before = jnp.dot(earlier, onehot, preferred_element_type=jnp.float32)
+    slot = jnp.sum(before * onehot.astype(jnp.float32), axis=1).astype(jnp.int32)
     return (flat * capacity + slot).reshape(route_block.shape)
 
 
@@ -67,12 +70,10 @@
     table = returned.reshape(-1, width)
     weights = combine_weights[0].reshape(micro * tok_count, topk)
     mixing = jnp.sum(jnp.where(hits, weights[..., None], 0.0), axis=1)
-    combined = jnp.dot(
-        mixing,
-        table.astype(jnp.float32),
-        precision=lax.Precision.HIGHEST,
-        preferred_element_type=jnp.float32,
-    )
+    high = lax.reduce_precision(mixing, exponent_bits=8, mantissa_bits=7)
+    low = (mixing - high).astype(jnp.bfloat16)
+    combined = jnp.dot(high.astype(jnp.bfloat16), table, preferred_element_type=jnp.float32)
+    combined = combined + jnp.dot(low, table, preferred_element_type=jnp.float32)
     mixed = inputs.astype(jnp.float32) + combined.reshape(micro, tok_count, width)
     moved = from_behind(mixed.astype(jnp.bfloat16), "section", 1)
     return moved[None]

time: 75.6 us -> 76.6 us (1.013)
  matrix products: 4.81 us -> 6.09 us
    dot_general x1 -> x2, matrix products: 1.67 us -> 2.83 us  [the longest x1 1.43 us: local(): jnp.dot(high.astype(jnp.bfloat16), table, preferred_element_type=jnp.floa...]
where the time goes in v8:
time: 76.6 us; the launch traced here: 76.3 us
  waiting for transfers between devices  30.5 us (40%)
  blocking collectives  26.3 us (34%)
  matrix products  6.09 us (8%)
  starting transfers between devices  5.93 us (8%)
  other arithmetic  4.39 us (6%)
  local copies, waits for them, and re-layouts  2.94 us (4%)
    all_to_all x1, blocking collectives, local(): lax.all_to_all(buffer, 'z', split_axis=0, concat_axis=0, tiled=True)  26.3 us
    all_to_all x1, waiting for transfers between devices, local(): lax.all_to_all(results, 'z', split_axis=0, concat_axis=0, tiled=True)  20.5 us
    ppermute x1, waiting for transfers between devices, from_behind(): return lax.ppermute(value, axis, pairs)  6.9 us
    all_to_all x1, starting transfers between devices, local(): lax.all_to_all(results, 'z', split_axis=0, concat_axis=0, tiled=True)  4.19 us
    ppermute x2, waiting for transfers between devices, swap_cores(): return lax.ppermute(value, 'core', [(0, 1), (1, 0)])  3.05 us
    unnamed x11, local copies, waits for them, and re-layouts  2.26 us
    dot_general x2, matrix products, expert_half(): joined = jnp.dot(token_rows, weights_gu, preferred_element_type=jnp.float32)  1.55 us
    ppermute x1, starting transfers between devices, from_behind(): return lax.ppermute(value, axis, pairs)  1.54 us
  transfers between devices with their start and end apart: 4, of which 4 were waited for; matrix products, arithmetic and copies ran while one was open for 2% of the time, Pallas kernels for 0%

profile of v8, /device:TPU:0, one launch (start us, length us, event | category | flops | bytes accessed | tf_op | source)
XLA Modules:
  0.0 76.3 jit_solution(12161407501693117817)
XLA Ops:
  0.0 0.9 %copy.20 = s32[1,2,32,2]{3,2,1,0:T(8,128)S(1)} copy(s32[1,2,32,2]{2,3,1,0:T(2,128)} %param.7) | data formatting | bytes 1024 | tf_op args[1]
  0.9 0.7 broadcast_multiply_fusion
  1.8 0.1 fusion.21
  1.9 0.1 convert_element_type.77
  2.5 1.1 %fusion.9 = f32[2,32]{1,0:T(2,128)S(1)} fusion(bf16[1,2,32,2048]{3,2,1,0:T(8,128)(2,1)} %param.6), kind=kLoop, calls=%fused_computation.17 | loop fusion | flops 393152 | bytes 262400 | tf_op jit(solution)/shard_map/reduce_sum | solution.py:33
  3.7 1.1 %fusion.8 = bf16[64,2048]{1,0:T(8,128)(2,1)S(1)} fusion(bf16[1,2,32,2048]{3,2,1,0:T(8,128)(2,1)} %param.6, f32[2048]{0:T(1024)} %bitcast.58, f32[64]{0:T(128)S(1)} %rsqrt.12), kind=kLoop, calls=%fused_computation.14 | loop fusion | flops 524288 | bytes 532736 | tf_op jit(solution)/shard_map/convert_element_type | solution.py:34
  4.8 0.4 convolution_convert_fusion
  5.2 26.3 %all_to_all.10 = bf16[4,48,2048]{2,1,0:T(8,128)(2,1)S(1)} all-to-all(bf16[4,48,2048]{2,1,0:T(8,128)(2,1)S(1)} %bitcast.52), channel_id=1, replica_groups=mesh['section'=4,'z'=4,'core'=2] {'z'}, dimensions={0} | all-to-all | bytes 1572864 | tf_op jit(solution)/shard_map/all_to_all | solution.py:62
  31.4 2.3 %collective-permute-done = bf16[4,48,2048]{2,1,0:T(8,128)(2,1)S(1)} collective-permute-done((bf16[4,48,2048]{2,1,0:T(8,128)(2,1)S(1)}, bf16[4,48,2048]{2,1,0:T(8,128)(2,1)S(1)}, u32[]{:S(2)}, u32[]{:S(2)}) %collective-permute-start) | collective-permute-done | bytes 786464 | tf_op jit(solution)/shard_map/ppermute | solution.py:17
  33.7 0.8 %fusion = f32[192,768]{1,0:T(8,128)S(1)} fusion(bf16[192,2048]{1,0:T(8,128)(2,1)S(1)} %bitcast.56, bf16[1,1,2048,768]{3,2,1,0:T(8,128)(2,1)S(1)} %copy-done), kind=kOutput, calls=%fused_computation | convolution fusion | flops 603979776 | bytes 4521984 | tf_op jit(solution)/shard_map/dot_general | solution.py:39
  34.5 0.6 copy-done.3
  35.1 0.6 convolution_convert_fusion.1
  35.7 0.2 collective-permute-start.1
  35.9 0.8 %fusion.2 = f32[192,768]{1,0:T(8,128)S(1)} fusion(bf16[192,2048]{1,0:T(8,128)(2,1)S(1)} %bitcast.53, bf16[1,1,2048,768]{3,2,1,0:T(8,128)(2,1)S(1)} %copy-done), kind=kOutput, calls=%fused_computation.2 | convolution fusion | flops 603979776 | bytes 4521984 | tf_op jit(solution)/shard_map/dot_general | solution.py:39
  36.7 0.6 convolution_convert_fusion.2
  37.3 0.8 %collective-permute-done.1 = bf16[4,48,2048]{2,1,0:T(8,128)(2,1)S(1)} collective-permute-done((bf16[4,48,2048]{2,1,0:T(8,128)(2,1)S(1)}, bf16[4,48,2048]{2,1,0:T(8,128)(2,1)S(1)}, u32[]{:S(2)}, u32[]{:S(2)}) %collective-permute-start.1) | collective-permute-done | bytes 786464 | tf_op jit(solution)/shard_map/ppermute | solution.py:17
  38.1 1.2 %fusion.4 = bf16[4,48,2048]{2,1,0:T(8,128)(2,1)} fusion(bf16[4,48,2048]{2,1,0:T(8,128)(2,1)S(1)} %bitcast.55, bf16[4,48,2048]{2,1,0:T(8,128)(2,1)S(1)} %collective-permute-done.1), kind=kLoop, calls=%fused_computation.9 | loop fusion | flops 1572864 | bytes 2359296 | tf_op jit(solution)/shard_map/convert_element_type | solution.py:68
  39.3 4.2 %all-to-all-start.1 = ((bf16[4,48,2048]{2,1,0:T(8,128)(2,1)}), bf16[4,48,2048]{2,1,0:T(8,128)(2,1)}, u32[]{:S(2)}, u32[]{:S(2)}) async-start(bf16[4,48,2048]{2,1,0:T(8,128)(2,1)} %fusion.4), calls=%async_computation.1 | async-start | bytes 1572864 | tf_op jit(solution)/shard_map/all_to_all | solution.py:69
  43.7 20.5 %all-to-all-done.1 = bf16[4,48,2048]{2,1,0:T(8,128)(2,1)} async-done(((bf16[4,48,2048]{2,1,0:T(8,128)(2,1)}), bf16[4,48,2048]{2,1,0:T(8,128)(2,1)}, u32[]{:S(2)}, u32[]{:S(2)}) %all-to-all-start.1) | async-done | bytes 786464 | tf_op jit(solution)/shard_map/all_to_all | solution.py:69
  64.2 1.4 %fusion.20 = f32[64,2048]{1,0:T(8,128)S(1)} fusion(bf16[192,2048]{1,0:T(8,128)(2,1)} %bitcast.14, f32[64,192]{1,0:T(8,128)S(1)} %select_reduce_fusion), kind=kOutput, calls=%fused_computation.31 | convolution fusion | flops 50356224 | bytes 1359872 | tf_op jit(solution)/shard_map/dot_general | solution.py:75
  65.6 1.4 %convolution_add_fusion = f32[64,2048]{1,0:T(8,128)S(1)} fusion(f32[64,2048]{1,0:T(8,128)S(1)} %fusion.20, bf16[192,2048]{1,0:T(8,128)(2,1)} %bitcast.14, f32[64,192]{1,0:T(8,128)S(1)} %select_reduce_fusion), kind=kOutput, calls=%fused_computation.7 | convolution fusion | flops 50499584 | bytes 1884160 | tf_op jit(solution)/shard_map/dot_general | solution.py:76
  67.1 1.5 %collective-permute-start.2 = (bf16[2,32,2048]{2,1,0:T(8,128)(2,1)S(1)}, bf16[2,32,2048]{2,1,0:T(8,128)(2,1)S(1)}, u32[]{:S(2)}, u32[]{:S(2)}) collective-permute-start(bf16[2,32,2048]{2,1,0:T(8,128)(2,1)S(1)} %fusion.10), channel_id=1, source_target_pairs={{0,8},{8,16},{16,24},{24,0},{1,9},{9,17},{17,25},{25,1},{2,10},{10... | collective-permute-start | bytes 786440 | tf_op jit(solution)/shard_map/ppermute | solution.py:13
  68.7 6.9 %collective-permute-done.2 = bf16[2,32,2048]{2,1,0:T(8,128)(2,1)S(1)} collective-permute-done((bf16[2,32,2048]{2,1,0:T(8,128)(2,1)S(1)}, bf16[2,32,2048]{2,1,0:T(8,128)(2,1)S(1)}, u32[]{:S(2)}, u32[]{:S(2)}) %collective-permute-start.2) | collective-permute-done | bytes 262176 | tf_op jit(solution)/shard_map/ppermute | solution.py:13
  75.6 0.7 copy.24
  (26 shorter events, 0.9 us)
Async XLA Ops:
  0.0 33.7 %copy-start = (bf16[1,1,2048,768]{3,2,1,0:T(8,128)(2,1)S(1)}, bf16[1,1,2048,768]{3,2,1,0:T(8,128)(2,1)}, u32[]{:S(2)}) copy-start(bf16[1,1,2048,768]{3,2,1,0:T(8,128)(2,1)} %param.10) | copy-start | bytes 9437188
  31.4 2.3 %collective-permute-start = (bf16[4,48,2048]{2,1,0:T(8,128)(2,1)S(1)}, bf16[4,48,2048]{2,1,0:T(8,128)(2,1)S(1)}, u32[]{:S(2)}, u32[]{:S(2)}) collective-permute-start(bf16[4,48,2048]{2,1,0:T(8,128)(2,1)S(1)} %all_to_all.10), channel_id=1, source_target_pairs={{0,1},{1,0},{2,3},{3,2},{4,5},{5,4},{6,7},{7,6},{8,9},{9,8},{10,11... | collective-permute-start | bytes 2359304 | tf_op jit(solution)/shard_map/ppermute | solution.py:17
  33.7 1.4 %copy-start.3 = (bf16[1,1,384,2048]{3,2,1,0:T(8,128)(2,1)S(1)}, bf16[1,1,384,2048]{3,2,1,0:T(8,128)(2,1)}, u32[]{:S(2)}) copy-start(bf16[1,1,384,2048]{3,2,1,0:T(8,128)(2,1)} %param.11) | copy-start | bytes 4718596
  35.7 2.4 %collective-permute-start.1 = (bf16[4,48,2048]{2,1,0:T(8,128)(2,1)S(1)}, bf16[4,48,2048]{2,1,0:T(8,128)(2,1)S(1)}, u32[]{:S(2)}, u32[]{:S(2)}) collective-permute-start(bf16[4,48,2048]{2,1,0:T(8,128)(2,1)S(1)} %bitcast.61), channel_id=1, source_target_pairs={{0,1},{1,0},{2,3},{3,2},{4,5},{5,4},{6,7},{7,6},{8,9},{9,8},{10,11... | collective-permute-start | bytes 2359304 | tf_op jit(solution)/shard_map/ppermute | solution.py:17
  38.1 5.4 %copy-start.2 = (f32[1,2,32,2]{2,3,1,0:T(2,128)S(1)}, f32[1,2,32,2]{2,3,1,0:T(2,128)}, u32[]{:S(2)}) copy-start(f32[1,2,32,2]{2,3,1,0:T(2,128)} %param.8) | copy-start | bytes 1540
  39.3 24.9 %all-to-all-start.1 = ((bf16[4,48,2048]{2,1,0:T(8,128)(2,1)}), bf16[4,48,2048]{2,1,0:T(8,128)(2,1)}, u32[]{:S(2)}, u32[]{:S(2)}) async-start(bf16[4,48,2048]{2,1,0:T(8,128)(2,1)} %fusion.4), calls=%async_computation.1 | async-start | bytes 1572864 | tf_op jit(solution)/shard_map/all_to_all | solution.py:69
  64.2 2.8 %copy-start.1 = (bf16[1,2,32,2048]{3,2,1,0:T(8,128)(2,1)S(1)}, bf16[1,2,32,2048]{3,2,1,0:T(8,128)(2,1)}, u32[]{:S(2)}) copy-start(bf16[1,2,32,2048]{3,2,1,0:T(8,128)(2,1)} %param.6) | copy-start | bytes 786436
  67.1 8.4 %collective-permute-start.2 = (bf16[2,32,2048]{2,1,0:T(8,128)(2,1)S(1)}, bf16[2,32,2048]{2,1,0:T(8,128)(2,1)S(1)}, u32[]{:S(2)}, u32[]{:S(2)}) collective-permute-start(bf16[2,32,2048]{2,1,0:T(8,128)(2,1)S(1)} %fusion.10), channel_id=1, source_target_pairs={{0,8},{8,16},{16,24},{24,0},{1,9},{9,17},{17,25},{25,1},{2,10},{10... | collective-permute-start | bytes 786440 | tf_op jit(solution)/shard_map/ppermute | solution.py:13

commit v9 on v5

v9 whole, which is shorter than its diff:
```python
import jax
import jax.numpy as jnp
from jax import lax
from jax.experimental import pallas as pl
from jax.sharding import Mesh
from jax.sharding import PartitionSpec as P

EPSILON = 1e-06


def from_behind(value, axis, steps):
    count = lax.axis_size(axis)
    pairs = [(source, (source + steps) % count) for source in range(count)]
    return lax.ppermute(value, axis, pairs)


def swap_cores(value):
    return lax.ppermute(value, "core", [(0, 1), (1, 0)])


def expert_half(token_rows, weights_gu, weights_dn):
    units = weights_dn.shape[0]
    joined = jnp.dot(token_rows, weights_gu, preferred_element_type=jnp.float32)
    hidden = (jax.nn.silu(joined[:, :units]) * joined[:, units:]).astype(jnp.bfloat16)
    partial_out = jnp.dot(hidden, weights_dn, preferred_element_type=jnp.float32)
    return partial_out.astype(jnp.bfloat16)


def prepare_kernel(x_ref, gain_ref, route_ref, weight_ref, buffer_ref, mixing_ref, *, micro, experts, capacity):
    rows, _ = x_ref.shape
    topk = route_ref.shape[1]
    tok_count = rows // micro
    block = micro * capacity
    slots = experts * block
    values = x_ref[...].astype(jnp.float32)
    scale = lax.rsqrt(jnp.mean(values * values, axis=-1, keepdims=True) + EPSILON)
    normed = (values * scale * gain_ref[...]).astype(jnp.bfloat16)
    routes = route_ref[...]
    weights = weight_ref[...]
    down_ix = lax.broadcasted_iota(jnp.int32, (rows, rows), 0)
    across = lax.broadcasted_iota(jnp.int32, (rows, rows), 1)
    group_down = jnp.zeros((rows, rows), jnp.int32)
    group_across = jnp.zeros((rows, rows), jnp.int32)
    group_row = jnp.zeros((rows, 1), jnp.int32)
    row_ix = lax.broadcasted_iota(jnp.int32, (rows, 1), 0)
    for m in range(1, micro):
        group_down = group_down + (down_ix >= m * tok_count).astype(jnp.int32)
        group_across = group_across + (across >= m * tok_count).astype(jnp.int32)
        group_row = group_row + (row_ix >= m * tok_count).astype(jnp.int32)
    earlier = ((group_down == group_across) & (across < down_ix)).astype(jnp.bfloat16)
    names = lax.broadcasted_iota(jnp.int32, (rows, experts), 1)
    picks = [(routes[:, k : k + 1] == names).astype(jnp.float32) for k in range(topk)]
    total = picks[0]
    for k in range(1, topk):
        total = total + picks[k]
    before = jnp.dot(earlier, total.astype(jnp.bfloat16), preferred_element_type=jnp.float32)
    lanes = lax.broadcasted_iota(jnp.int32, (rows, slots), 1)
    hit = jnp.zeros((rows, slots), jnp.float32)
    mixing = jnp.zeros((rows, slots), jnp.float32)
    for k in range(topk):
        slot = jnp.sum(before * picks[k], axis=1, keepdims=True).astype(jnp.int32)
        place = routes[:, k : k + 1] * block + group_row * capacity + slot
        match = place == lanes
        hit = jnp.maximum(hit, match.astype(jnp.float32))
        mixing = mixing + jnp.where(match, weights[:, k : k + 1], 0.0)
        before = before + picks[k]
    buffer = lax.dot_general(
        hit.astype(jnp.bfloat16),
        normed,
        (((0,), (0,)), ((), ())),
        preferred_element_type=jnp.float32,
    )
    buffer_ref[...] = buffer.astype(jnp.bfloat16)
    mixing_ref[...] = mixing


def prepare(inputs, gain, routes, weights, experts, capacity):
    micro, tok_count, width = inputs.shape
    rows = micro * tok_count
    slots = experts * micro * capacity
    return pl.pallas_call(
        lambda *refs: prepare_kernel(*refs, micro=micro, experts=experts, capacity=capacity),
        out_shape=(
            jax.ShapeDtypeStruct((slots, width), jnp.bfloat16),
            jax.ShapeDtypeStruct((rows, slots), jnp.float32),
        ),
    )(inputs.reshape(rows, width), gain.reshape(1, width), routes.reshape(rows, -1), weights.reshape(rows, -1))


def body(tokens, routes, combine_weights, norm_gain, gate_up, down):
    inputs = tokens[0]
    micro, tok_count, width = inputs.shape
    experts = lax.axis_size("z")
    topk = routes.shape[3]
    capacity = 2 * ((3 * tok_count * topk + 4 * experts - 1) // (4 * experts))
    block = micro * capacity
    buffer, mixing = prepare(inputs, norm_gain[0], routes[0], combine_weights[0], experts, capacity)
    buffer = buffer.reshape(experts, block, width)
    incoming = lax.all_to_all(buffer, "z", split_axis=0, concat_axis=0, tiled=True)
    partner_rows = swap_cores(incoming)
    own = expert_half(incoming.reshape(-1, width), gate_up[0, 0], down[0, 0])
    lent = expert_half(partner_rows.reshape(-1, width), gate_up[0, 0], down[0, 0])
    other_half = swap_cores(lent.reshape(incoming.shape))
    results = (own.reshape(incoming.shape).astype(jnp.float32) + other_half.astype(jnp.float32))
    results = results.astype(jnp.bfloat16)
    returned = lax.all_to_all(results, "z", split_axis=0, concat_axis=0, tiled=True)
    table = returned.reshape(-1, width)
    combined = jnp.dot(
        mixing,
        table.astype(jnp.float32),
        precision=lax.Precision.HIGHEST,
        preferred_element_type=jnp.float32,
    )
    mixed = inputs.astype(jnp.float32) + combined.reshape(micro, tok_count, width)
    moved = from_behind(mixed.astype(jnp.bfloat16), "section", 1)
    return moved[None]


def solution(mesh):
    sections, spread = mesh.devices.shape
    chips = Mesh(mesh.devices.reshape(sections, spread // 2, 2), ("section", "z", "core"))
    split = ("z", "core")
    return jax.shard_map(
        body,
        mesh=chips,
        in_specs=(
            P("section", None, split, None),
            P("section", None, split, None),
            P("section", None, split, None),
            P("section", None),
            P("section", split, None, None),
            P("section", split, None, None),
        ),
        out_specs=P("section", None, split, None),
        check_vma=False,
    )
```

time: 75.6 us -> 71.9 us (0.951)
  blocking collectives: 26.3 us -> 49.6 us
  waiting for transfers between devices: 30.5 us -> 9.85 us
  other arithmetic: 4.68 us -> 0.26 us
  starting transfers between devices: 5.93 us -> 1.74 us
  Pallas kernels: 0 us -> 2.63 us
  matrix products: 4.81 us -> 3.27 us
  local copies, waits for them, and re-layouts: 2.94 us -> 4.23 us
    all_to_all x1 -> x2, blocking collectives: 26.3 us -> 49.6 us  [the longest x1 26.5 us: body(): lax.all_to_all(buffer, 'z', split_axis=0, concat_axis=0, tiled=True)]
    all_to_all x1 -> x0, waiting for transfers between devices: 20.5 us -> none  [local(): lax.all_to_all(results, 'z', split_axis=0, concat_axis=0, tiled=True)]
    all_to_all x1 -> x0, starting transfers between devices: 4.19 us -> none  [local(): lax.all_to_all(results, 'z', split_axis=0, concat_axis=0, tiled=True)]
    another operation x0 -> x2, local copies, waits for them, and re-layouts: none -> 2.89 us  [the longest x1 1.52 us: prepare(): routes.reshape(rows, -1)]
    pallas_call x0 -> x1, Pallas kernels: none -> 2.63 us  [prepare(): pl.pallas_call(lambda *refs: prepare_kernel(*refs, micro=micro, experts=e...]
    convert_element_type x3 -> x1, other arithmetic: 2.36 us -> 0.26 us  [body(): results = results.astype(jnp.bfloat16)]
    dot_general x2 -> x1, matrix products: 2.07 us -> 0.54 us  [body(): jnp.dot(mixing, table.astype(jnp.float32), precision=lax.Precision.HIGHES...]
    reduce_sum x3 -> x0, other arithmetic: 1.36 us -> none  [the longest x1 1.08 us: normalize(): jnp.mean(values * values, axis=-1, keepdims=True) + EPSILON]
  transfers between devices with their start and end apart: 4 -> 3, of which waited for: 4 -> 3; matrix products, arithmetic and copies ran while one was open for 2% -> 2% of each run, Pallas kernels for 0% -> 0%
where the time goes in v9:
time: 71.9 us; the launch traced here: 71.6 us
  blocking collectives  49.6 us (69%)
  waiting for transfers between devices  9.85 us (14%)
  local copies, waits for them, and re-layouts  4.23 us (6%)
  matrix products  3.27 us (5%)
  Pallas kernels  2.63 us (4%)
  starting transfers between devices  1.74 us (2%)
    all_to_all x1, blocking collectives, body(): lax.all_to_all(buffer, 'z', split_axis=0, concat_axis=0, tiled=True)  26.5 us
    all_to_all x1, blocking collectives, body(): lax.all_to_all(results, 'z', split_axis=0, concat_axis=0, tiled=True)  23.1 us
    ppermute x1, waiting for transfers between devices, from_behind(): return lax.ppermute(value, axis, pairs)  6.8 us
    ppermute x2, waiting for transfers between devices, swap_cores(): return lax.ppermute(value, 'core', [(0, 1), (1, 0)])  3.05 us
    pallas_call x1, Pallas kernels, prepare(): pl.pallas_call(lambda *refs: prepare_kernel(*refs, micro=micro, experts=e...  2.63 us
    dot_general x2, matrix products, expert_half(): joined = jnp.dot(token_rows, weights_gu, preferred_element_type=jnp.float32)  1.55 us
    ppermute x1, starting transfers between devices, from_behind(): return lax.ppermute(value, axis, pairs)  1.53 us
    another operation x1, local copies, waits for them, and re-layouts, prepare(): routes.reshape(rows, -1)  1.52 us
  transfers between devices with their start and end apart: 3, of which 3 were waited for; matrix products, arithmetic and copies ran while one was open for 2% of the time, Pallas kernels for 0%

profile of v9, /device:TPU:0, one launch (start us, length us, event | category | flops | bytes accessed | tf_op | source)
XLA Modules:
  0.0 71.6 jit_solution(476185348007540319)
XLA Ops:
  0.0 0.0 copy-start
  0.0 1.5 %copy.11 = s32[1,2,32,2]{3,2,1,0:T(8,128)} copy(s32[1,2,32,2]{2,3,1,0:T(2,128)} %param.7) | data formatting | bytes 1024 | tf_op jit(solution)/shard_map/reshape;squeeze | solution.py:87
  1.5 1.4 %copy.12 = f32[1,2,32,2]{3,2,1,0:T(8,128)} copy(f32[1,2,32,2]{2,3,1,0:T(2,128)} %param.8) | data formatting | bytes 1024 | tf_op jit(solution)/shard_map/reshape;squeeze | solution.py:87
  2.9 2.6 %shard_map.64 = (bf16[192,2048]{1,0:T(8,128)(2,1)}, f32[64,192]{1,0:T(8,128)}) custom-call(bf16[64,2048]{1,0:T(8,128)(2,1)} %bitcast.33, f32[1,2048]{1,0:T(1,128)} %refs_1_.1, s32[64,2]{1,0:T(8,128)} %bitcast.38, f32[64,2]{1,0:T(8,128)} %bitcast.39), custom_call_target="tpu_custom_call" | custom-call | tf_op jit(solution)/shard_map/pallas_call | solution.py:81
  5.5 26.5 %all_to_all.10 = bf16[4,48,2048]{2,1,0:T(8,128)(2,1)S(1)} all-to-all(bf16[4,48,2048]{2,1,0:T(8,128)(2,1)} %bitcast.34), channel_id=1, replica_groups=mesh['section'=4,'z'=4,'core'=2] {'z'}, dimensions={0} | all-to-all | bytes 1572864 | tf_op jit(solution)/shard_map/all_to_all | solution.py:99
  32.0 0.0 collective-permute-start
  32.0 2.3 %collective-permute-done = bf16[4,48,2048]{2,1,0:T(8,128)(2,1)S(1)} collective-permute-done((bf16[4,48,2048]{2,1,0:T(8,128)(2,1)S(1)}, bf16[4,48,2048]{2,1,0:T(8,128)(2,1)S(1)}, u32[]{:S(2)}, u32[]{:S(2)}) %collective-permute-start) | collective-permute-done | bytes 786464 | tf_op jit(solution)/shard_map/ppermute | solution.py:18
  34.3 0.0 copy-done
  34.3 0.0 copy-start.3
  34.3 0.8 %fusion = f32[192,768]{1,0:T(8,128)S(1)} fusion(bf16[192,2048]{1,0:T(8,128)(2,1)S(1)} %bitcast.36, bf16[1,1,2048,768]{3,2,1,0:T(8,128)(2,1)S(1)} %copy-done), kind=kOutput, calls=%fused_computation | convolution fusion | flops 603979776 | bytes 4521984 | tf_op jit(solution)/shard_map/dot_general | solution.py:23
  35.1 0.6 copy-done.3
  35.7 0.6 convolution_convert_fusion
  36.3 0.2 collective-permute-start.1
  36.5 0.8 %fusion.2 = f32[192,768]{1,0:T(8,128)S(1)} fusion(bf16[192,2048]{1,0:T(8,128)(2,1)S(1)} %bitcast.32, bf16[1,1,2048,768]{3,2,1,0:T(8,128)(2,1)S(1)} %copy-done), kind=kOutput, calls=%fused_computation.2 | convolution fusion | flops 603979776 | bytes 4521984 | tf_op jit(solution)/shard_map/dot_general | solution.py:23
  37.3 0.6 convolution_convert_fusion.1
  37.9 0.8 %collective-permute-done.1 = bf16[4,48,2048]{2,1,0:T(8,128)(2,1)S(1)} collective-permute-done((bf16[4,48,2048]{2,1,0:T(8,128)(2,1)S(1)}, bf16[4,48,2048]{2,1,0:T(8,128)(2,1)S(1)}, u32[]{:S(2)}, u32[]{:S(2)}) %collective-permute-start.1) | collective-permute-done | bytes 786464 | tf_op jit(solution)/shard_map/ppermute | solution.py:18
  38.6 0.3 fusion.5
  38.9 23.1 %all_to_all.11 = bf16[4,48,2048]{2,1,0:T(8,128)(2,1)S(1)} all-to-all(bf16[4,48,2048]{2,1,0:T(8,128)(2,1)S(1)} %fusion.5), channel_id=1, replica_groups=mesh['section'=4,'z'=4,'core'=2] {'z'}, dimensions={0} | all-to-all | bytes 1572864 | tf_op jit(solution)/shard_map/all_to_all | solution.py:106
  62.0 0.0 copy-done.1
  62.0 0.0 copy-done.2
  62.0 0.5 fusion.4
  62.6 1.5 %collective-permute-start.2 = (bf16[2,32,2048]{2,1,0:T(8,128)(2,1)S(1)}, bf16[2,32,2048]{2,1,0:T(8,128)(2,1)S(1)}, u32[]{:S(2)}, u32[]{:S(2)}) collective-permute-start(bf16[2,32,2048]{2,1,0:T(8,128)(2,1)S(1)} %fusion.4), channel_id=1, source_target_pairs={{0,8},{8,16},{16,24},{24,0},{1,9},{9,17},{17,25},{25,1},{2,10},{10... | collective-permute-start | bytes 786440 | tf_op jit(solution)/shard_map/ppermute | solution.py:14
  64.1 6.8 %collective-permute-done.2 = bf16[2,32,2048]{2,1,0:T(8,128)(2,1)S(1)} collective-permute-done((bf16[2,32,2048]{2,1,0:T(8,128)(2,1)S(1)}, bf16[2,32,2048]{2,1,0:T(8,128)(2,1)S(1)}, u32[]{:S(2)}, u32[]{:S(2)}) %collective-permute-start.2) | collective-permute-done | bytes 262176 | tf_op jit(solution)/shard_map/ppermute | solution.py:14
  70.9 0.7 copy.16
  (2 shorter events, 0.0 us)
Async XLA Ops:
  0.0 34.3 %copy-start = (bf16[1,1,2048,768]{3,2,1,0:T(8,128)(2,1)S(1)}, bf16[1,1,2048,768]{3,2,1,0:T(8,128)(2,1)}, u32[]{:S(2)}) copy-start(bf16[1,1,2048,768]{3,2,1,0:T(8,128)(2,1)} %param.10) | copy-start | bytes 9437188
  32.0 2.3 %collective-permute-start = (bf16[4,48,2048]{2,1,0:T(8,128)(2,1)S(1)}, bf16[4,48,2048]{2,1,0:T(8,128)(2,1)S(1)}, u32[]{:S(2)}, u32[]{:S(2)}) collective-permute-start(bf16[4,48,2048]{2,1,0:T(8,128)(2,1)S(1)} %all_to_all.10), channel_id=1, source_target_pairs={{0,1},{1,0},{2,3},{3,2},{4,5},{5,4},{6,7},{7,6},{8,9},{9,8},{10,11... | collective-permute-start | bytes 2359304 | tf_op jit(solution)/shard_map/ppermute | solution.py:18
  34.3 1.4 %copy-start.3 = (bf16[1,1,384,2048]{3,2,1,0:T(8,128)(2,1)S(1)}, bf16[1,1,384,2048]{3,2,1,0:T(8,128)(2,1)}, u32[]{:S(2)}) copy-start(bf16[1,1,384,2048]{3,2,1,0:T(8,128)(2,1)} %param.11) | copy-start | bytes 4718596
  36.3 2.4 %collective-permute-start.1 = (bf16[4,48,2048]{2,1,0:T(8,128)(2,1)S(1)}, bf16[4,48,2048]{2,1,0:T(8,128)(2,1)S(1)}, u32[]{:S(2)}, u32[]{:S(2)}) collective-permute-start(bf16[4,48,2048]{2,1,0:T(8,128)(2,1)S(1)} %bitcast.41), channel_id=1, source_target_pairs={{0,1},{1,0},{2,3},{3,2},{4,5},{5,4},{6,7},{7,6},{8,9},{9,8},{10,11... | collective-permute-start | bytes 2359304 | tf_op jit(solution)/shard_map/ppermute | solution.py:18
  38.6 23.4 %copy-start.1 = (bf16[1,2,32,2048]{3,2,1,0:T(8,128)(2,1)S(1)}, bf16[1,2,32,2048]{3,2,1,0:T(8,128)(2,1)}, u32[]{:S(2)}) copy-start(bf16[1,2,32,2048]{3,2,1,0:T(8,128)(2,1)} %param.6) | copy-start | bytes 786436
  38.6 23.4 %copy-start.2 = (f32[64,192]{1,0:T(8,128)S(1)}, f32[64,192]{1,0:T(8,128)}, u32[]{:S(2)}) copy-start(f32[64,192]{1,0:T(8,128)} %get-tuple-element.7) | copy-start | bytes 147460
  62.6 8.3 %collective-permute-start.2 = (bf16[2,32,2048]{2,1,0:T(8,128)(2,1)S(1)}, bf16[2,32,2048]{2,1,0:T(8,128)(2,1)S(1)}, u32[]{:S(2)}, u32[]{:S(2)}) collective-permute-start(bf16[2,32,2048]{2,1,0:T(8,128)(2,1)S(1)} %fusion.4), channel_id=1, source_target_pairs={{0,8},{8,16},{16,24},{24,0},{1,9},{9,17},{17,25},{25,1},{2,10},{10... | collective-permute-start | bytes 786440 | tf_op jit(solution)/shard_map/ppermute | solution.py:14
